TPU v7x, 256 devices: a whole 4x4x8 slice. The times are simulated.
256 devices in a mesh: ctx: 16 (over z_lo, x), ch: 16 (over y, z_hi, core).
Axes of the slice: x: 4, y: 4, z: 8 (z_hi: 2, z_lo: 4; z = z_hi * 4 + z_lo), core: 2. Of those that a mesh axis runs over, the one named last changes fastest.
Arguments:
- tokens: bfloat16 [4096, 8192], P('ctx', 'ch'), may hold values from -6 to 6
- in_weight: bfloat16 [8192, 3, 8192], P('ctx', None, 'ch'), may hold values from -0.0625 to 0.0625
- short_filter: bfloat16 [3, 3, 8192], P(None, None, 'ch'), may hold values from -3 to 3
- decay_rate: float32 [8192, 16], P('ch'), may hold values from 1.2207031e-05 to 0.0333333333
- residue: float32 [8192, 16], P('ch'), may hold values from -0.12 to 0.12
- skip_gain: float32 [8192], P('ch'), may hold values from -4 to 4
Outputs:
- filtered: bfloat16 [4096, 8192], P('ctx', 'ch')
All inputs are finite; a program needn't handle non-finite values.
Results may differ from a plain program's by a relative error of at most 0.007.
Values may be sent and summed in bfloat16 or wider, within the bound.
No kernel may reach another device: no remote copies, remote signals or barrier semaphores. Data moves between devices by JAX's collectives and lax.ppermute only.
A program may use at most 128 MiB of HBM per device.

v0:
```python
import jax
import jax.numpy as jnp
import numpy as np
from jax import lax
from jax.sharding import Mesh, PartitionSpec as P

exact_mode = lax.Precision.HIGHEST
SEQ = ("zl", "x")
SUB = ("zh", "c")
CH = ("y", "zh", "c")


def from_behind(block, axis, distance):
    devices = range(lax.axis_size(axis))
    route = [(i - distance, i) for i in devices if i - distance in devices]
    return lax.ppermute(block, axis, route)


def ring_sends(pieces, axis, size):
    position = lax.axis_index(axis)
    received = []
    for k in range(1, size):
        route = [(i, (i + k) % size) for i in range(size)]
        received.append(lax.ppermute(pieces(k, position), axis, route))
    return received


def line_gather(piece, axis, size):
    below, above = [], []
    near_b = lax.ppermute(piece, axis, [(i, i + 1) for i in range(size - 1)])
    near_a = lax.ppermute(piece, axis, [(i + 1, i) for i in range(size - 1)])
    below.append(near_b)
    above.append(near_a)
    for d in range(2, size):
        near_b = lax.ppermute(near_b, axis, [(i, i + 1) for i in range(d - 1, size - 1)])
        near_a = lax.ppermute(near_a, axis, [(i + 1, i) for i in range(0, size - d)])
        below.append(near_b)
        above.append(near_a)
    return below, above


def block(tokens, in_weight, short_filter, decay_rate, residue, skip_gain):
    tok_rows = tokens.shape[0]
    width_local = in_weight.shape[2]
    mode_count = decay_rate.shape[1]
    feat_block = in_weight.shape[0]
    across, down = lax.axis_size("x"), lax.axis_size("zl")
    me_x, me_z = lax.axis_index("x"), lax.axis_index("zl")
    halves = lax.axis_size("zh")
    pair = lax.axis_size("c")
    me_h = lax.axis_index("zh")
    stream_count = in_weight.shape[1]
    order = tuple(range(1, stream_count)) + (0,)
    relays = {}
    for s in order:
        relays[s] = line_gather(in_weight[:, s, :], "zl", down)
    swap = [(a * across + b, b * across + a) for a in range(across) for b in range(across)]
    cross = [
        (a * across + b, b * across + ((a // pair + 1) % halves) * pair + a % pair)
        for a in range(across)
        for b in range(across)
    ]
    near = lax.ppermute(tokens, ("x",) + SUB, swap)
    far = lax.ppermute(tokens, ("x",) + SUB, cross)
    both = jnp.stack([jnp.where(me_h == 0, near, far), jnp.where(me_h == 0, far, near)])
    gathered = lax.all_gather(both, ("y", "c"), axis=0, tiled=False)
    blocks = gathered.reshape(-1, pair, halves, tok_rows, feat_block)

    def contribution(source, weight):
        taken = lax.dynamic_index_in_dim(blocks, source, axis=0, keepdims=False)
        return jnp.einsum("chru,uk->hcrk", taken, weight, preferred_element_type=jnp.float32)

    reduced = {}
    for s in order:
        below, above = relays[s]
        partial = contribution(me_z, in_weight[:, s, :])
        for d in range(1, down):
            low, high = jnp.maximum(me_z - d, 0), jnp.minimum(me_z + d, down - 1)
            if 2 * d <= down - 1:
                partial = partial + contribution(low, below[d - 1])
                partial = partial + contribution(high, above[d - 1])
            else:
                use_low = me_z - d >= 0
                weight = jnp.where(use_low, below[d - 1], above[d - 1])
                partial = partial + contribution(jnp.where(use_low, low, high), weight)
        partial = partial.reshape(across, tok_rows, width_local)
        total = lax.dynamic_index_in_dim(partial, me_x, axis=0, keepdims=False)
        for k in range(1, across):
            route = [(i, (i + k) % across) for i in range(across)]
            piece = lax.dynamic_index_in_dim(partial, (me_x + k) % across, axis=0, keepdims=False)
            total = total + lax.ppermute(piece, "x", route)
        reduced[s] = total
    tap_count = short_filter.shape[0]
    filter_taps = short_filter.astype(jnp.float32)

    def short_conv(group):
        streams = jnp.stack([reduced[t] for t in group], axis=1).astype(jnp.bfloat16)
        last_rows = streams[tok_rows - (tap_count - 1) :]
        before = from_behind(last_rows, SEQ, 1)
        padded = jnp.concatenate([before, streams], axis=0).astype(jnp.float32)
        taps = filter_taps[:, group[0] : group[-1] + 1]
        featured = jnp.zeros((tok_rows, len(group), width_local), jnp.float32)
        for shift_back in range(tap_count):
            begin = tap_count - 1 - shift_back
            featured = featured + taps[shift_back][None] * padded[begin : begin + tok_rows]
        return featured

    gates = short_conv(order[:-1])
    gated_rows = (gates[:, 0] * gates[:, 1]).astype(jnp.bfloat16)
    gated_wide = gated_rows.astype(jnp.float32)
    position = jnp.arange(tok_rows, dtype=jnp.float32)
    powers = jnp.exp(-decay_rate[None, :, :] * (tok_rows - 1.0 - position)[:, None, None])
    local_state = jnp.einsum("jc,jcr->cr", gated_wide, powers, precision=exact_mode)
    along = [local_state] + ring_sends(lambda k, p: local_state, "x", across)
    row = jnp.stack(along)
    states = jnp.stack([row] + ring_sends(lambda k, p: row, "zl", down))
    step_z = jnp.arange(down)[:, None]
    step_x = jnp.arange(across)[None, :]
    source = ((me_z - step_z) % down) * across + (me_x - step_x) % across
    lag = (me_z * across + me_x - 1 - source).astype(jnp.float32)
    decay_b = decay_rate[None, None]
    weight = jnp.exp(-decay_b * (float(tok_rows) * jnp.maximum(lag, 0.0))[:, :, None, None])
    weight = jnp.where((lag >= 0)[:, :, None, None], weight, 0.0)
    incoming = jnp.sum(weight * states, axis=(0, 1))
    growth = jnp.exp(decay_rate[None, :, :] * position[:, None, None])
    scaled = (gated_wide[:, :, None] * growth).reshape(tok_rows, width_local * mode_count)
    lower_mask = (jnp.arange(tok_rows)[:, None] >= jnp.arange(tok_rows)[None, :]).astype(
        jnp.float32
    )
    running_sum = jnp.dot(lower_mask, scaled, precision=exact_mode).reshape(
        tok_rows, width_local, mode_count
    )
    shrink = jnp.exp(-decay_rate[None, :, :] * position[:, None, None])
    weighted = residue[None] * shrink
    inside = jnp.sum(weighted * running_sum, axis=2)
    entering = (incoming * jnp.exp(-decay_rate))[None]
    convolved = inside + jnp.sum(weighted * entering, axis=2)
    long_mix = convolved + skip_gain[None, :] * gated_wide
    query_gate = short_conv(order[-1:])[:, 0]
    return (query_gate * long_mix).astype(jnp.bfloat16)


def split_mesh(mesh):
    ctx, ch = mesh.shape["ctx"], mesh.shape["ch"]
    devices = np.asarray(mesh.devices).reshape(ctx // 4, 4, ch // 4, 2, 2)
    return Mesh(devices, SEQ + CH)


def solution(mesh):
    fine = split_mesh(mesh)
    in_specs = (
        P(SEQ, CH),
        P(SEQ, None, CH),
        P(None, None, CH),
        P(CH, None),
        P(CH, None),
        P(CH),
    )
    out_specs = P(SEQ, CH)
    return jax.shard_map(block, mesh=fine, in_specs=in_specs, out_specs=out_specs, check_vma=False)
```

profile of v0, /device:TPU:32, one launch (start us, length us, event | category | flops | bytes accessed | tf_op | source)
XLA Modules:
  0.0 246.2 jit_solution(4679603063530477387)
XLA Ops:
  8.3 8.8 %collective-permute-start.1 = (bf16[256,512]{1,0:T(8,128)(2,1)}, bf16[256,512]{1,0:T(8,128)(2,1)S(1)}, u32[]{:S(2)}, u32[]{:S(2)}) collective-permute-start(bf16[256,512]{1,0:T(8,128)(2,1)} %param.6), channel_id=1, source_target_pairs={{0,2},{1,18},{2,34},{3,50},{16,3},{17,19},{18,35},{19,51},{32,0},{... | collective-permute-start | bytes 786440 | tf_op jit(solution)/shard_map/ppermute | solution.py:64
  17.0 7.3 %collective-permute-done.1 = bf16[256,512]{1,0:T(8,128)(2,1)S(1)} collective-permute-done((bf16[256,512]{1,0:T(8,128)(2,1)}, bf16[256,512]{1,0:T(8,128)(2,1)S(1)}, u32[]{:S(2)}, u32[]{:S(2)}) %collective-permute-start.1) | collective-permute-done | bytes 262176 | tf_op jit(solution)/shard_map/ppermute | solution.py:64
  26.6 6.8 %collective-permute-start.2 = (bf16[512,512]{1,0:T(8,128)(2,1)}, bf16[512,512]{1,0:T(8,128)(2,1)}, u32[]{:S(2)}, u32[]{:S(2)}) collective-permute-start(bf16[512,512]{1,0:T(8,128)(2,1)} %get-tuple-element.17), channel_id=1, source_target_pairs={{0,64},{64,128},{128,192},{1,65},{65,129},{129,193},{2,66},{66,130... | collective-permute-start | bytes 1572872 | tf_op jit(solution)/shard_map/ppermute | solution.py:30
  35.3 3.9 %collective-permute-start.21 = (bf16[512,512]{1,0:T(8,128)(2,1)}, bf16[512,512]{1,0:T(8,128)(2,1)S(1)}, u32[]{:S(2)}, u32[]{:S(2)}) collective-permute-start(bf16[512,512]{1,0:T(8,128)(2,1)} %get-tuple-element.18), channel_id=1, source_target_pairs={{0,64},{64,128},{128,192},{1,65},{65,129},{129,193},{2,66},{66,130... | collective-permute-start | bytes 1572872 | tf_op jit(solution)/shard_map/ppermute | solution.py:30
  41.2 3.9 %collective-permute-start.12 = (bf16[512,512]{1,0:T(8,128)(2,1)}, bf16[512,512]{1,0:T(8,128)(2,1)S(1)}, u32[]{:S(2)}, u32[]{:S(2)}) collective-permute-start(bf16[512,512]{1,0:T(8,128)(2,1)} %get-tuple-element.16), channel_id=1, source_target_pairs={{0,64},{64,128},{128,192},{1,65},{65,129},{129,193},{2,66},{66,130... | collective-permute-start | bytes 1572872 | tf_op jit(solution)/shard_map/ppermute | solution.py:30
  45.7 20.8 %all-gather.3.cloned.1.call-done = bf16[16,256,512]{2,1,0:T(8,128)(2,1)} async-done(((bf16[2,256,512]{2,1,0:T(8,128)(2,1)}), bf16[16,256,512]{2,1,0:T(8,128)(2,1)}) %all-gather.3.cloned.1.call-update) | async-done | bytes 4194320 | tf_op jit(solution)/shard_map/all_gather | solution.py:66
  72.9 3.4 %collective-permute-start.4 = (bf16[512,512]{1,0:T(8,128)(2,1)}, bf16[512,512]{1,0:T(8,128)(2,1)S(1)}, u32[]{:S(2)}, u32[]{:S(2)}) collective-permute-start(bf16[512,512]{1,0:T(8,128)(2,1)} %collective-permute-done.2), channel_id=1, source_target_pairs={{64,128},{128,192},{65,129},{129,193},{66,130},{130,194},{67,131},... | collective-permute-start | bytes 1572872 | tf_op jit(solution)/shard_map/ppermute | solution.py:35
  78.3 4.0 %collective-permute-start.23 = (bf16[512,512]{1,0:T(8,128)(2,1)S(1)}, bf16[512,512]{1,0:T(8,128)(2,1)S(1)}, u32[]{:S(2)}, u32[]{:S(2)}) collective-permute-start(bf16[512,512]{1,0:T(8,128)(2,1)S(1)} %collective-permute-done.21), channel_id=1, source_target_pairs={{64,128},{128,192},{65,129},{129,193},{66,130},{130,194},{67,131},... | collective-permute-start | bytes 1572872 | tf_op jit(solution)/shard_map/ppermute | solution.py:35
  87.4 3.3 %collective-permute-start.14 = (bf16[512,512]{1,0:T(8,128)(2,1)S(1)}, bf16[512,512]{1,0:T(8,128)(2,1)S(1)}, u32[]{:S(2)}, u32[]{:S(2)}) collective-permute-start(bf16[512,512]{1,0:T(8,128)(2,1)S(1)} %collective-permute-done.12), channel_id=1, source_target_pairs={{64,128},{128,192},{65,129},{129,193},{66,130},{130,194},{67,131},... | collective-permute-start | bytes 1572872 | tf_op jit(solution)/shard_map/ppermute | solution.py:35
  92.7 6.0 %collective-permute-done.5 = bf16[512,512]{1,0:T(8,128)(2,1)S(1)} collective-permute-done((bf16[512,512]{1,0:T(8,128)(2,1)}, bf16[512,512]{1,0:T(8,128)(2,1)S(1)}, u32[]{:S(2)}, u32[]{:S(2)}) %collective-permute-start.5) | collective-permute-done | bytes 524320 | tf_op jit(solution)/shard_map/ppermute | solution.py:36
  104.3 5.6 %collective-permute-done.24 = bf16[512,512]{1,0:T(8,128)(2,1)S(1)} collective-permute-done((bf16[512,512]{1,0:T(8,128)(2,1)S(1)}, bf16[512,512]{1,0:T(8,128)(2,1)S(1)}, u32[]{:S(2)}, u32[]{:S(2)}) %collective-permute-start.24) | collective-permute-done | bytes 524320 | tf_op jit(solution)/shard_map/ppermute | solution.py:36
  113.0 7.3 %collective-permute-done.15 = bf16[512,512]{1,0:T(8,128)(2,1)S(1)} collective-permute-done((bf16[512,512]{1,0:T(8,128)(2,1)S(1)}, bf16[512,512]{1,0:T(8,128)(2,1)S(1)}, u32[]{:S(2)}, u32[]{:S(2)}) %collective-permute-start.15) | collective-permute-done | bytes 524320 | tf_op jit(solution)/shard_map/ppermute | solution.py:36
  124.3 6.1 %collective-permute-done.7 = bf16[512,512]{1,0:T(8,128)(2,1)S(1)} collective-permute-done((bf16[512,512]{1,0:T(8,128)(2,1)S(1)}, bf16[512,512]{1,0:T(8,128)(2,1)S(1)}, u32[]{:S(2)}, u32[]{:S(2)}) %collective-permute-start.7) | collective-permute-done | bytes 524320 | tf_op jit(solution)/shard_map/ppermute | solution.py:36
  138.1 3.5 %collective-permute-done.26 = bf16[512,512]{1,0:T(8,128)(2,1)S(1)} collective-permute-done((bf16[512,512]{1,0:T(8,128)(2,1)S(1)}, bf16[512,512]{1,0:T(8,128)(2,1)S(1)}, u32[]{:S(2)}, u32[]{:S(2)}) %collective-permute-start.26) | collective-permute-done | bytes 524320 | tf_op jit(solution)/shard_map/ppermute | solution.py:36
  147.6 4.5 %collective-permute-done.17 = bf16[512,512]{1,0:T(8,128)(2,1)S(1)} collective-permute-done((bf16[512,512]{1,0:T(8,128)(2,1)S(1)}, bf16[512,512]{1,0:T(8,128)(2,1)S(1)}, u32[]{:S(2)}, u32[]{:S(2)}) %collective-permute-start.17) | collective-permute-done | bytes 524320 | tf_op jit(solution)/shard_map/ppermute | solution.py:36
  156.9 3.5 %collective-permute-start.20 = (f32[256,512]{1,0:T(8,128)S(1)}, f32[256,512]{1,0:T(8,128)S(1)}, u32[]{:S(2)}, u32[]{:S(2)}) collective-permute-start(f32[256,512]{1,0:T(8,128)S(1)} %get-tuple-element.8), channel_id=1, source_target_pairs={{0,48},{16,0},{32,16},{48,32},{1,49},{17,1},{33,17},{49,33},{2,50}... | collective-permute-start | bytes 1572872 | tf_op jit(solution)/shard_map/ppermute | solution.py:91
  160.4 4.5 %collective-permute-done.8 = f32[256,512]{1,0:T(8,128)S(1)} collective-permute-done((f32[256,512]{1,0:T(8,128)S(1)}, f32[256,512]{1,0:T(8,128)S(1)}, u32[]{:S(2)}, u32[]{:S(2)}) %collective-permute-start.8) | collective-permute-done | bytes 524320 | tf_op jit(solution)/shard_map/ppermute | solution.py:91
  165.7 12.7 %collective-permute-done.29 = f32[256,512]{1,0:T(8,128)S(1)} collective-permute-done((f32[256,512]{1,0:T(8,128)S(1)}, f32[256,512]{1,0:T(8,128)S(1)}, u32[]{:S(2)}, u32[]{:S(2)}) %collective-permute-start.29) | collective-permute-done | bytes 524320 | tf_op jit(solution)/shard_map/ppermute | solution.py:91
  178.7 5.8 %collective-permute-start.11 = (bf16[2,1,512]{2,0,1:T(2,128)(2,1)S(1)}, bf16[2,1,512]{2,0,1:T(2,128)(2,1)S(1)}, u32[]{:S(2)}, u32[]{:S(2)}) collective-permute-start(bf16[2,1,512]{2,0,1:T(2,128)(2,1)S(1)} %slice_bitcast_fusion.6), channel_id=1, source_target_pairs={{0,16},{16,32},{32,48},{48,64},{64,80},{80,96},{96,112},{112,128},... | collective-permute-start | bytes 6152 | tf_op jit(solution)/shard_map/ppermute | solution.py:16
  184.5 9.0 %collective-permute-done.27 = f32[256,512]{1,0:T(8,128)S(1)} collective-permute-done((f32[256,512]{1,0:T(8,128)S(1)}, f32[256,512]{1,0:T(8,128)S(1)}, u32[]{:S(2)}, u32[]{:S(2)}) %collective-permute-start.27) | collective-permute-done | bytes 524320 | tf_op jit(solution)/shard_map/ppermute | solution.py:91
  193.7 6.8 %collective-permute-done.20 = f32[256,512]{1,0:T(8,128)S(1)} collective-permute-done((f32[256,512]{1,0:T(8,128)S(1)}, f32[256,512]{1,0:T(8,128)S(1)}, u32[]{:S(2)}, u32[]{:S(2)}) %collective-permute-start.20) | collective-permute-done | bytes 524320 | tf_op jit(solution)/shard_map/ppermute | solution.py:91
  200.5 6.7 %collective-permute-done.18 = f32[256,512]{1,0:T(8,128)S(1)} collective-permute-done((f32[256,512]{1,0:T(8,128)S(1)}, f32[256,512]{1,0:T(8,128)S(1)}, u32[]{:S(2)}, u32[]{:S(2)}) %collective-permute-start.18) | collective-permute-done | bytes 524320 | tf_op jit(solution)/shard_map/ppermute | solution.py:91
  209.5 5.6 %collective-permute-done.30 = bf16[2,2,512]{2,0,1:T(2,128)(2,1)S(1)} collective-permute-done((bf16[2,2,512]{2,0,1:T(2,128)(2,1)S(1)}, bf16[2,2,512]{2,0,1:T(2,128)(2,1)S(1)}, u32[]{:S(2)}, u32[]{:S(2)}) %collective-permute-start.30) | collective-permute-done | bytes 4128 | tf_op jit(solution)/shard_map/ppermute | solution.py:16
  226.6 9.7 %multiply_reduce_fusion.2 = f32[256,512]{1,0:T(8,128)S(1)} fusion(f32[512,16]{0,1:T(8,128)S(1)} %neg.8, f32[512,16]{0,1:T(8,128)S(1)} %copy-done.5, f32[512,16,256]{2,1,0:T(8,128)S(1)} %bitcast.266), kind=kOutput, calls=%fused_computation.5 | convolution fusion | flops 6450774016 | bytes 8978432 | tf_op jit(solution)/shard_map/dot_general | solution.py:130
  (118 shorter events, 72.4 us)
Async XLA Ops:
  6.5 59.9 %all-gather.3.cloned.1.call-start = ((), (), s32[]{:S(2)}) async-start(), calls=%async_computation | async-start | bytes 4718592 | tf_op jit(solution)/shard_map/all_gather | solution.py:66
  26.6 43.9 %collective-permute-start.2 = (bf16[512,512]{1,0:T(8,128)(2,1)}, bf16[512,512]{1,0:T(8,128)(2,1)}, u32[]{:S(2)}, u32[]{:S(2)}) collective-permute-start(bf16[512,512]{1,0:T(8,128)(2,1)} %get-tuple-element.17), channel_id=1, source_target_pairs={{0,64},{64,128},{128,192},{1,65},{65,129},{129,193},{2,66},{66,130... | collective-permute-start | bytes 1572872 | tf_op jit(solution)/shard_map/ppermute | solution.py:30
  33.4 39.6 %collective-permute-start.3 = (bf16[512,512]{1,0:T(8,128)(2,1)}, bf16[512,512]{1,0:T(8,128)(2,1)}, u32[]{:S(2)}, u32[]{:S(2)}) collective-permute-start(bf16[512,512]{1,0:T(8,128)(2,1)} %get-tuple-element.17), channel_id=1, source_target_pairs={{64,0},{128,64},{192,128},{65,1},{129,65},{193,129},{66,2},{130,66... | collective-permute-start | bytes 1572872 | tf_op jit(solution)/shard_map/ppermute | solution.py:31
  35.3 41.1 %collective-permute-start.21 = (bf16[512,512]{1,0:T(8,128)(2,1)}, bf16[512,512]{1,0:T(8,128)(2,1)S(1)}, u32[]{:S(2)}, u32[]{:S(2)}) collective-permute-start(bf16[512,512]{1,0:T(8,128)(2,1)} %get-tuple-element.18), channel_id=1, source_target_pairs={{0,64},{64,128},{128,192},{1,65},{65,129},{129,193},{2,66},{66,130... | collective-permute-start | bytes 1572872 | tf_op jit(solution)/shard_map/ppermute | solution.py:30
  39.2 39.1 %collective-permute-start.22 = (bf16[512,512]{1,0:T(8,128)(2,1)}, bf16[512,512]{1,0:T(8,128)(2,1)S(1)}, u32[]{:S(2)}, u32[]{:S(2)}) collective-permute-start(bf16[512,512]{1,0:T(8,128)(2,1)} %get-tuple-element.18), channel_id=1, source_target_pairs={{64,0},{128,64},{192,128},{65,1},{129,65},{193,129},{66,2},{130,66... | collective-permute-start | bytes 1572872 | tf_op jit(solution)/shard_map/ppermute | solution.py:31
  41.2 43.6 %collective-permute-start.12 = (bf16[512,512]{1,0:T(8,128)(2,1)}, bf16[512,512]{1,0:T(8,128)(2,1)S(1)}, u32[]{:S(2)}, u32[]{:S(2)}) collective-permute-start(bf16[512,512]{1,0:T(8,128)(2,1)} %get-tuple-element.16), channel_id=1, source_target_pairs={{0,64},{64,128},{128,192},{1,65},{65,129},{129,193},{2,66},{66,130... | collective-permute-start | bytes 1572872 | tf_op jit(solution)/shard_map/ppermute | solution.py:30
  84.8 25.1 %collective-permute-start.24 = (bf16[512,512]{1,0:T(8,128)(2,1)S(1)}, bf16[512,512]{1,0:T(8,128)(2,1)S(1)}, u32[]{:S(2)}, u32[]{:S(2)}) collective-permute-start(bf16[512,512]{1,0:T(8,128)(2,1)S(1)} %collective-permute-done.22), channel_id=1, source_target_pairs={{64,0},{128,64},{65,1},{129,65},{66,2},{130,66},{67,3},{131,67},{6... | collective-permute-start | bytes 1572872 | tf_op jit(solution)/shard_map/ppermute | solution.py:36
  87.4 23.2 %collective-permute-start.14 = (bf16[512,512]{1,0:T(8,128)(2,1)S(1)}, bf16[512,512]{1,0:T(8,128)(2,1)S(1)}, u32[]{:S(2)}, u32[]{:S(2)}) collective-permute-start(bf16[512,512]{1,0:T(8,128)(2,1)S(1)} %collective-permute-done.12), channel_id=1, source_target_pairs={{64,128},{128,192},{65,129},{129,193},{66,130},{130,194},{67,131},... | collective-permute-start | bytes 1572872 | tf_op jit(solution)/shard_map/ppermute | solution.py:35
  90.7 29.6 %collective-permute-start.15 = (bf16[512,512]{1,0:T(8,128)(2,1)S(1)}, bf16[512,512]{1,0:T(8,128)(2,1)S(1)}, u32[]{:S(2)}, u32[]{:S(2)}) collective-permute-start(bf16[512,512]{1,0:T(8,128)(2,1)S(1)} %collective-permute-done.13), channel_id=1, source_target_pairs={{64,0},{128,64},{65,1},{129,65},{66,2},{130,66},{67,3},{131,67},{6... | collective-permute-start | bytes 1572872 | tf_op jit(solution)/shard_map/ppermute | solution.py:36
  98.6 22.4 %collective-permute-start.6 = (bf16[512,512]{1,0:T(8,128)(2,1)S(1)}, bf16[512,512]{1,0:T(8,128)(2,1)S(1)}, u32[]{:S(2)}, u32[]{:S(2)}) collective-permute-start(bf16[512,512]{1,0:T(8,128)(2,1)S(1)} %collective-permute-done.4), channel_id=1, source_target_pairs={{128,192},{129,193},{130,194},{131,195},{132,196},{133,197},{134,1... | collective-permute-start | bytes 1572872 | tf_op jit(solution)/shard_map/ppermute | solution.py:35
  100.1 30.3 %collective-permute-start.7 = (bf16[512,512]{1,0:T(8,128)(2,1)S(1)}, bf16[512,512]{1,0:T(8,128)(2,1)S(1)}, u32[]{:S(2)}, u32[]{:S(2)}) collective-permute-start(bf16[512,512]{1,0:T(8,128)(2,1)S(1)} %collective-permute-done.5), channel_id=1, source_target_pairs={{64,0},{65,1},{66,2},{67,3},{68,4},{69,5},{70,6},{71,7},{72,8},{73... | collective-permute-start | bytes 1572872 | tf_op jit(solution)/shard_map/ppermute | solution.py:36
  109.9 27.3 %collective-permute-start.25 = (bf16[512,512]{1,0:T(8,128)(2,1)S(1)}, bf16[512,512]{1,0:T(8,128)(2,1)S(1)}, u32[]{:S(2)}, u32[]{:S(2)}) collective-permute-start(bf16[512,512]{1,0:T(8,128)(2,1)S(1)} %collective-permute-done.23), channel_id=1, source_target_pairs={{128,192},{129,193},{130,194},{131,195},{132,196},{133,197},{134,1... | collective-permute-start | bytes 1572872 | tf_op jit(solution)/shard_map/ppermute | solution.py:35
  110.6 31.0 %collective-permute-start.26 = (bf16[512,512]{1,0:T(8,128)(2,1)S(1)}, bf16[512,512]{1,0:T(8,128)(2,1)S(1)}, u32[]{:S(2)}, u32[]{:S(2)}) collective-permute-start(bf16[512,512]{1,0:T(8,128)(2,1)S(1)} %collective-permute-done.24), channel_id=1, source_target_pairs={{64,0},{65,1},{66,2},{67,3},{68,4},{69,5},{70,6},{71,7},{72,8},{73... | collective-permute-start | bytes 1572872 | tf_op jit(solution)/shard_map/ppermute | solution.py:36
  120.4 25.3 %collective-permute-start.16 = (bf16[512,512]{1,0:T(8,128)(2,1)S(1)}, bf16[512,512]{1,0:T(8,128)(2,1)S(1)}, u32[]{:S(2)}, u32[]{:S(2)}) collective-permute-start(bf16[512,512]{1,0:T(8,128)(2,1)S(1)} %collective-permute-done.14), channel_id=1, source_target_pairs={{128,192},{129,193},{130,194},{131,195},{132,196},{133,197},{134,1... | collective-permute-start | bytes 1572872 | tf_op jit(solution)/shard_map/ppermute | solution.py:35
  121.1 31.0 %collective-permute-start.17 = (bf16[512,512]{1,0:T(8,128)(2,1)S(1)}, bf16[512,512]{1,0:T(8,128)(2,1)S(1)}, u32[]{:S(2)}, u32[]{:S(2)}) collective-permute-start(bf16[512,512]{1,0:T(8,128)(2,1)S(1)} %collective-permute-done.15), channel_id=1, source_target_pairs={{64,0},{65,1},{66,2},{67,3},{68,4},{69,5},{70,6},{71,7},{72,8},{73... | collective-permute-start | bytes 1572872 | tf_op jit(solution)/shard_map/ppermute | solution.py:36
  131.6 24.5 %collective-permute-start.10 = (f32[256,512]{1,0:T(8,128)S(1)}, f32[256,512]{1,0:T(8,128)S(1)}, u32[]{:S(2)}, u32[]{:S(2)}) collective-permute-start(f32[256,512]{1,0:T(8,128)S(1)} %get-tuple-element.14), channel_id=1, source_target_pairs={{0,48},{16,0},{32,16},{48,32},{1,49},{17,1},{33,17},{49,33},{2,50}... | collective-permute-start | bytes 1572872 | tf_op jit(solution)/shard_map/ppermute | solution.py:91
  141.6 23.3 %collective-permute-start.8 = (f32[256,512]{1,0:T(8,128)S(1)}, f32[256,512]{1,0:T(8,128)S(1)}, u32[]{:S(2)}, u32[]{:S(2)}) collective-permute-start(f32[256,512]{1,0:T(8,128)S(1)} %get-tuple-element.13), channel_id=1, source_target_pairs={{0,16},{16,32},{32,48},{48,0},{1,17},{17,33},{33,49},{49,1},{2,18}... | collective-permute-start | bytes 1572872 | tf_op jit(solution)/shard_map/ppermute | solution.py:91
  145.7 32.7 %collective-permute-start.29 = (f32[256,512]{1,0:T(8,128)S(1)}, f32[256,512]{1,0:T(8,128)S(1)}, u32[]{:S(2)}, u32[]{:S(2)}) collective-permute-start(f32[256,512]{1,0:T(8,128)S(1)} %get-tuple-element.11), channel_id=1, source_target_pairs={{0,48},{16,0},{32,16},{48,32},{1,49},{17,1},{33,17},{49,33},{2,50}... | collective-permute-start | bytes 1572872 | tf_op jit(solution)/shard_map/ppermute | solution.py:91
  152.1 26.6 %collective-permute-start.28 = (f32[256,512]{1,0:T(8,128)S(1)}, f32[256,512]{1,0:T(8,128)S(1)}, u32[]{:S(2)}, u32[]{:S(2)}) collective-permute-start(f32[256,512]{1,0:T(8,128)S(1)} %get-tuple-element.12), channel_id=1, source_target_pairs={{0,32},{16,48},{32,0},{48,16},{1,33},{17,49},{33,1},{49,17},{2,34}... | collective-permute-start | bytes 1572872 | tf_op jit(solution)/shard_map/ppermute | solution.py:91
  156.1 37.4 %collective-permute-start.27 = (f32[256,512]{1,0:T(8,128)S(1)}, f32[256,512]{1,0:T(8,128)S(1)}, u32[]{:S(2)}, u32[]{:S(2)}) collective-permute-start(f32[256,512]{1,0:T(8,128)S(1)} %get-tuple-element.10), channel_id=1, source_target_pairs={{0,16},{16,32},{32,48},{48,0},{1,17},{17,33},{33,49},{49,1},{2,18}... | collective-permute-start | bytes 1572872 | tf_op jit(solution)/shard_map/ppermute | solution.py:91
  156.9 43.6 %collective-permute-start.20 = (f32[256,512]{1,0:T(8,128)S(1)}, f32[256,512]{1,0:T(8,128)S(1)}, u32[]{:S(2)}, u32[]{:S(2)}) collective-permute-start(f32[256,512]{1,0:T(8,128)S(1)} %get-tuple-element.8), channel_id=1, source_target_pairs={{0,48},{16,0},{32,16},{48,32},{1,49},{17,1},{33,17},{49,33},{2,50}... | collective-permute-start | bytes 1572872 | tf_op jit(solution)/shard_map/ppermute | solution.py:91
  164.9 35.6 %collective-permute-start.19 = (f32[256,512]{1,0:T(8,128)S(1)}, f32[256,512]{1,0:T(8,128)S(1)}, u32[]{:S(2)}, u32[]{:S(2)}) collective-permute-start(f32[256,512]{1,0:T(8,128)S(1)} %get-tuple-element.9), channel_id=1, source_target_pairs={{0,32},{16,48},{32,0},{48,16},{1,33},{17,49},{33,1},{49,17},{2,34}... | collective-permute-start | bytes 1572872 | tf_op jit(solution)/shard_map/ppermute | solution.py:91
  178.4 28.8 %collective-permute-start.18 = (f32[256,512]{1,0:T(8,128)S(1)}, f32[256,512]{1,0:T(8,128)S(1)}, u32[]{:S(2)}, u32[]{:S(2)}) collective-permute-start(f32[256,512]{1,0:T(8,128)S(1)} %get-tuple-element.7), channel_id=1, source_target_pairs={{0,16},{16,32},{32,48},{48,0},{1,17},{17,33},{33,49},{49,1},{2,18}... | collective-permute-start | bytes 1572872 | tf_op jit(solution)/shard_map/ppermute | solution.py:91
  178.7 30.7 %collective-permute-start.11 = (bf16[2,1,512]{2,0,1:T(2,128)(2,1)S(1)}, bf16[2,1,512]{2,0,1:T(2,128)(2,1)S(1)}, u32[]{:S(2)}, u32[]{:S(2)}) collective-permute-start(bf16[2,1,512]{2,0,1:T(2,128)(2,1)S(1)} %slice_bitcast_fusion.6), channel_id=1, source_target_pairs={{0,16},{16,32},{32,48},{48,64},{64,80},{80,96},{96,112},{112,128},... | collective-permute-start | bytes 6152 | tf_op jit(solution)/shard_map/ppermute | solution.py:16
  (20 other events, 269.2 us)
Sparse Core Ops, SparseCore 0:
  25.5 40.9 all-gather.2
where the time goes:
time: 248 us; the launch traced here: 246 us
  waiting for transfers between devices  111 us (45%)
  starting transfers between devices  84.8 us (34%)
  matrix products  25.5 us (10%)
  between operations  14.2 us (6%)
  other arithmetic  8.11 us (3%)
  local copies, waits for them, and re-layouts  2.63 us (1%)
    ppermute x9, waiting for transfers between devices, block(): total = total + lax.ppermute(piece, 'x', route)  39.7 us
    ppermute x6, waiting for transfers between devices, line_gather(): lax.ppermute(near_a, axis, [(i + 1, i) for i in range(0, size - d)])  33 us
    all_gather x1, waiting for transfers between devices, block(): gathered = lax.all_gather(both, ('y', 'c'), axis=0, tiled=False)  20.8 us
    dot_general x15, matrix products, contribution(): jnp.einsum('chru,uk->hcrk', taken, weight, preferred_element_type=jnp.flo...  15.8 us
    ppermute x9, starting transfers between devices, block(): total = total + lax.ppermute(piece, 'x', route)  14.9 us
    ppermute x3, starting transfers between devices, line_gather(): near_b = lax.ppermute(piece, axis, [(i, i + 1) for i in range(size - 1)])  14.6 us
    ppermute x6, starting transfers between devices, line_gather(): lax.ppermute(near_a, axis, [(i + 1, i) for i in range(0, size - d)])  13.1 us
    ppermute x6, starting transfers between devices, line_gather(): lax.ppermute(near_b, axis, [(i, i + 1) for i in range(d - 1, size - 1)])  12.8 us
  transfers between devices with their start and end apart: 38, of which 19 were waited for; matrix products, arithmetic and copies ran while one was open for 12% of the time, Pallas kernels for 0%

commit v1 on v0

--- a/solution.py
+++ b/solution.py
@@ -50,10 +50,11 @@
     pair = lax.axis_size("c")
     me_h = lax.axis_index("zh")
     stream_count = in_weight.shape[1]
-    order = tuple(range(1, stream_count)) + (0,)
+    order = (tuple(range(1, stream_count)), (0,))
     relays = {}
     for s in order:
-        relays[s] = line_gather(in_weight[:, s, :], "zl", down)
+        own = in_weight[:, s[0] : s[-1] + 1, :].reshape(feat_block, len(s) * width_local)
+        relays[s] = (own, line_gather(own, "zl", down))
     swap = [(a * across + b, b * across + a) for a in range(across) for b in range(across)]
     cross = [
         (a * across + b, b * across + ((a // pair + 1) % halves) * pair + a % pair)
@@ -72,8 +73,8 @@
 
     reduced = {}
     for s in order:
-        below, above = relays[s]
-        partial = contribution(me_z, in_weight[:, s, :])
+        own, (below, above) = relays[s]
+        partial = contribution(me_z, own)
         for d in range(1, down):
             low, high = jnp.maximum(me_z - d, 0), jnp.minimum(me_z + d, down - 1)
             if 2 * d <= down - 1:
@@ -83,13 +84,14 @@
                 use_low = me_z - d >= 0
                 weight = jnp.where(use_low, below[d - 1], above[d - 1])
                 partial = partial + contribution(jnp.where(use_low, low, high), weight)
-        partial = partial.reshape(across, tok_rows, width_local)
+        partial = partial.reshape(across, tok_rows, len(s) * width_local)
         total = lax.dynamic_index_in_dim(partial, me_x, axis=0, keepdims=False)
         for k in range(1, across):
             route = [(i, (i + k) % across) for i in range(across)]
             piece = lax.dynamic_index_in_dim(partial, (me_x + k) % across, axis=0, keepdims=False)
             total = total + lax.ppermute(piece, "x", route)
-        reduced[s] = total
+        for n, t in enumerate(s):
+            reduced[t] = total[:, n * width_local : (n + 1) * width_local]
     tap_count = short_filter.shape[0]
     filter_taps = short_filter.astype(jnp.float32)
 
@@ -105,7 +107,7 @@
             featured = featured + taps[shift_back][None] * padded[begin : begin + tok_rows]
         return featured
 
-    gates = short_conv(order[:-1])
+    gates = short_conv(order[0])
     gated_rows = (gates[:, 0] * gates[:, 1]).astype(jnp.bfloat16)
     gated_wide = gated_rows.astype(jnp.float32)
     position = jnp.arange(tok_rows, dtype=jnp.float32)
@@ -131,12 +133,10 @@
         tok_rows, width_local, mode_count
     )
     shrink = jnp.exp(-decay_rate[None, :, :] * position[:, None, None])
-    weighted = residue[None] * shrink
-    inside = jnp.sum(weighted * running_sum, axis=2)
     entering = (incoming * jnp.exp(-decay_rate))[None]
-    convolved = inside + jnp.sum(weighted * entering, axis=2)
+    convolved = jnp.sum(residue[None] * shrink * (running_sum + entering), axis=2)
     long_mix = convolved + skip_gain[None, :] * gated_wide
-    query_gate = short_conv(order[-1:])[:, 0]
+    query_gate = short_conv(order[1])[:, 0]
     return (query_gate * long_mix).astype(jnp.bfloat16)
 
 

time: 248 us -> 262 us (1.056)
  waiting for transfers between devices: 111 us -> 119 us
  matrix products: 25.5 us -> 31.2 us
  local copies, waits for them, and re-layouts: 2.63 us -> 7.01 us
    ppermute x6 -> x4, waiting for transfers between devices: 0.79 us -> 25.6 us  [line_gather(): lax.ppermute(near_b, axis, [(i, i + 1) for i in range(d - 1, size - 1)])]
    all_gather x1, waiting for transfers between devices: 20.8 us -> 0.01 us  [block(): gathered = lax.all_gather(both, ('y', 'c'), axis=0, tiled=False)]
    ppermute x3 -> x2, waiting for transfers between devices: 0.01 us -> 15 us  [line_gather(): near_b = lax.ppermute(piece, axis, [(i, i + 1) for i in range(size - 1)])]
    ppermute x6 -> x4, waiting for transfers between devices: 33 us -> 20.4 us  [line_gather(): lax.ppermute(near_a, axis, [(i + 1, i) for i in range(0, size - d)])]
    ppermute x9 -> x6, waiting for transfers between devices: 39.7 us -> 45.4 us  [block(): total = total + lax.ppermute(piece, 'x', route)]
    ppermute x6, starting transfers between devices: 4.94 us -> 10.6 us  [ring_sends(): received.append(lax.ppermute(pieces(k, position), axis, route))]
    ppermute x2, waiting for transfers between devices: 5.6 us -> 0.01 us  [from_behind(): return lax.ppermute(block, axis, route)]
    dot_general x15 -> x10, matrix products: 15.8 us -> 21.2 us  [contribution(): jnp.einsum('chru,uk->hcrk', taken, weight, preferred_element_type=jnp.flo...]
  transfers between devices with their start and end apart: 38 -> 29, of which waited for: 19 -> 12; matrix products, arithmetic and copies ran while one was open for 12% -> 12% of each run, Pallas kernels for 0% -> 0%
where the time goes in v1:
time: 262 us; the launch traced here: 261 us
  waiting for transfers between devices  119 us (45%)
  starting transfers between devices  83.3 us (32%)
  matrix products  31.2 us (12%)
  between operations  14 us (5%)
  local copies, waits for them, and re-layouts  7.01 us (3%)
  other arithmetic  6.34 us (2%)
    ppermute x6, waiting for transfers between devices, block(): total = total + lax.ppermute(piece, 'x', route)  45.4 us
    ppermute x4, waiting for transfers between devices, line_gather(): lax.ppermute(near_b, axis, [(i, i + 1) for i in range(d - 1, size - 1)])  25.6 us
    dot_general x10, matrix products, contribution(): jnp.einsum('chru,uk->hcrk', taken, weight, preferred_element_type=jnp.flo...  21.2 us
    ppermute x4, waiting for transfers between devices, line_gather(): lax.ppermute(near_a, axis, [(i + 1, i) for i in range(0, size - d)])  20.4 us
    ppermute x6, starting transfers between devices, block(): total = total + lax.ppermute(piece, 'x', route)  20.1 us
    ppermute x2, waiting for transfers between devices, line_gather(): near_b = lax.ppermute(piece, axis, [(i, i + 1) for i in range(size - 1)])  15 us
    ppermute x4, starting transfers between devices, line_gather(): lax.ppermute(near_b, axis, [(i, i + 1) for i in range(d - 1, size - 1)])  13.8 us
    ppermute x2, starting transfers between devices, line_gather(): near_b = lax.ppermute(piece, axis, [(i, i + 1) for i in range(size - 1)])  10.7 us
  transfers between devices with their start and end apart: 29, of which 12 were waited for; matrix products, arithmetic and copies ran while one was open for 12% of the time, Pallas kernels for 0%

profile of v1, /device:TPU:32, one launch (start us, length us, event | category | flops | bytes accessed | tf_op | source)
XLA Modules:
  0.0 261.2 jit_solution(17142152162347727103)
XLA Ops:
  8.1 8.8 %collective-permute-start.1 = (bf16[256,512]{1,0:T(8,128)(2,1)}, bf16[256,512]{1,0:T(8,128)(2,1)S(1)}, u32[]{:S(2)}, u32[]{:S(2)}) collective-permute-start(bf16[256,512]{1,0:T(8,128)(2,1)} %param.6), channel_id=1, source_target_pairs={{0,2},{1,18},{2,34},{3,50},{16,3},{17,19},{18,35},{19,51},{32,0},{... | collective-permute-start | bytes 786440 | tf_op jit(solution)/shard_map/ppermute | solution.py:65
  16.9 7.3 %collective-permute-done.1 = bf16[256,512]{1,0:T(8,128)(2,1)S(1)} collective-permute-done((bf16[256,512]{1,0:T(8,128)(2,1)}, bf16[256,512]{1,0:T(8,128)(2,1)S(1)}, u32[]{:S(2)}, u32[]{:S(2)}) %collective-permute-start.1) | collective-permute-done | bytes 262176 | tf_op jit(solution)/shard_map/ppermute | solution.py:65
  26.7 6.8 %collective-permute-start.12 = (bf16[512,1024]{1,0:T(8,128)(2,1)S(1)}, bf16[512,1024]{1,0:T(8,128)(2,1)S(1)}, u32[]{:S(2)}, u32[]{:S(2)}) collective-permute-start(bf16[512,1024]{1,0:T(8,128)(2,1)S(1)} %bitcast.194), channel_id=1, source_target_pairs={{0,64},{64,128},{128,192},{1,65},{65,129},{129,193},{2,66},{66,130... | collective-permute-start | bytes 3145736 | tf_op jit(solution)/shard_map/ppermute | solution.py:30
  37.3 3.9 %collective-permute-start.2 = (bf16[512,512]{1,0:T(8,128)(2,1)}, bf16[512,512]{1,0:T(8,128)(2,1)}, u32[]{:S(2)}, u32[]{:S(2)}) collective-permute-start(bf16[512,512]{1,0:T(8,128)(2,1)} %slice_bitcast_fusion), channel_id=1, source_target_pairs={{0,64},{64,128},{128,192},{1,65},{65,129},{129,193},{2,66},{66,130... | collective-permute-start | bytes 1572872 | tf_op jit(solution)/shard_map/ppermute | solution.py:30
  41.2 2.7 %collective-permute-start.3 = (bf16[512,512]{1,0:T(8,128)(2,1)}, bf16[512,512]{1,0:T(8,128)(2,1)}, u32[]{:S(2)}, u32[]{:S(2)}) collective-permute-start(bf16[512,512]{1,0:T(8,128)(2,1)} %slice_bitcast_fusion), channel_id=1, source_target_pairs={{64,0},{128,64},{192,128},{65,1},{129,65},{193,129},{66,2},{130,66... | collective-permute-start | bytes 1572872 | tf_op jit(solution)/shard_map/ppermute | solution.py:31
  43.9 13.1 %collective-permute-done.12 = bf16[512,1024]{1,0:T(8,128)(2,1)S(1)} collective-permute-done((bf16[512,1024]{1,0:T(8,128)(2,1)S(1)}, bf16[512,1024]{1,0:T(8,128)(2,1)S(1)}, u32[]{:S(2)}, u32[]{:S(2)}) %collective-permute-start.12) | collective-permute-done | bytes 1048608 | tf_op jit(solution)/shard_map/ppermute | solution.py:30
  57.0 5.4 %collective-permute-start.14 = (bf16[512,1024]{1,0:T(8,128)(2,1)S(1)}, bf16[512,1024]{1,0:T(8,128)(2,1)}, u32[]{:S(2)}, u32[]{:S(2)}) collective-permute-start(bf16[512,1024]{1,0:T(8,128)(2,1)S(1)} %collective-permute-done.12), channel_id=1, source_target_pairs={{64,128},{128,192},{65,129},{129,193},{66,130},{130,194},{67,131},... | collective-permute-start | bytes 3145736 | tf_op jit(solution)/shard_map/ppermute | solution.py:35
  68.3 5.2 %collective-permute-start.4 = (bf16[512,512]{1,0:T(8,128)(2,1)}, bf16[512,512]{1,0:T(8,128)(2,1)}, u32[]{:S(2)}, u32[]{:S(2)}) collective-permute-start(bf16[512,512]{1,0:T(8,128)(2,1)} %collective-permute-done.2), channel_id=1, source_target_pairs={{64,128},{128,192},{65,129},{129,193},{66,130},{130,194},{67,131},... | collective-permute-start | bytes 1572872 | tf_op jit(solution)/shard_map/ppermute | solution.py:35
  75.5 25.6 %collective-permute-done.4 = bf16[512,512]{1,0:T(8,128)(2,1)} collective-permute-done((bf16[512,512]{1,0:T(8,128)(2,1)}, bf16[512,512]{1,0:T(8,128)(2,1)}, u32[]{:S(2)}, u32[]{:S(2)}) %collective-permute-start.4) | collective-permute-done | bytes 524320 | tf_op jit(solution)/shard_map/ppermute | solution.py:35
  102.6 2.6 %collective-permute-done.5 = bf16[512,512]{1,0:T(8,128)(2,1)} collective-permute-done((bf16[512,512]{1,0:T(8,128)(2,1)}, bf16[512,512]{1,0:T(8,128)(2,1)}, u32[]{:S(2)}, u32[]{:S(2)}) %collective-permute-start.5) | collective-permute-done | bytes 524320 | tf_op jit(solution)/shard_map/ppermute | solution.py:36
  105.2 3.0 %collective-permute-start.7 = (bf16[512,512]{1,0:T(8,128)(2,1)}, bf16[512,512]{1,0:T(8,128)(2,1)}, u32[]{:S(2)}, u32[]{:S(2)}) collective-permute-start(bf16[512,512]{1,0:T(8,128)(2,1)} %collective-permute-done.5), channel_id=1, source_target_pairs={{64,0},{65,1},{66,2},{67,3},{68,4},{69,5},{70,6},{71,7},{72,8},{73... | collective-permute-start | bytes 1572872 | tf_op jit(solution)/shard_map/ppermute | solution.py:36
  112.3 2.6 %fusion.16 = f32[2,2,256,1024]{3,2,1,0:T(8,128)S(1)} fusion(bf16[512,1024,1,1]{1,0,2,3:T(8,128)(2,1)S(1)} %reshape.202, bf16[4,2,2,256,512]{4,3,2,1,0:T(8,128)(2,1)} %bitcast.178, s32[]{:T(128)S(6)} %select_n.135), kind=kOutput, calls=%fused_computation.25 | convolution fusion | flops 1073741824 | bytes 6291460 | tf_op jit(solution)/shard_map/chru,uk->hcrk/dot_general | solution.py:72
  120.4 2.5 fusion.7
  123.0 17.7 %collective-permute-done.17 = bf16[512,1024]{1,0:T(8,128)(2,1)} collective-permute-done((bf16[512,1024]{1,0:T(8,128)(2,1)}, bf16[512,1024]{1,0:T(8,128)(2,1)}, u32[]{:S(2)}, u32[]{:S(2)}) %collective-permute-start.17) | collective-permute-done | bytes 1048608 | tf_op jit(solution)/shard_map/ppermute | solution.py:36
  140.7 3.2 %bitcast_add_fusion = f32[2,2,256,1024]{3,2,0,1:T(8,128)S(1)} fusion(f32[1024,2,2,256]{0,3,2,1:T(8,128)S(1)} %fusion.7, f32[2,2,256,1024]{3,2,1,0:T(8,128)S(1)} %fusion.9, f32[2,2,256,1024]{3,2,1,0:T(8,128)S(1)} %fusion.16, f32[2,2,256,1024]{3,2,1,0:T(8,128)S(1)} %fusion.11, bf16[512,1024]{1,0:T(8,128)(2,1)} %collective-permute-done.16, ...), kind=kOutput, calls=%fused_computation.5 | convolution fusion | flops 1078460416 | bytes 24117252 | tf_op jit(solution)/shard_map/chru,uk->hcrk/dot_general | solution.py:72
  145.0 9.0 %collective-permute-start.19 = (f32[256,1024]{1,0:T(8,128)S(1)}, f32[256,1024]{1,0:T(8,128)S(1)}, u32[]{:S(2)}, u32[]{:S(2)}) collective-permute-start(f32[256,1024]{1,0:T(8,128)S(1)} %get-tuple-element.9), channel_id=1, source_target_pairs={{0,32},{16,48},{32,0},{48,16},{1,33},{17,49},{33,1},{49,17},{2,34}... | collective-permute-start | bytes 3145736 | tf_op jit(solution)/shard_map/ppermute | solution.py:92
  166.2 30.5 %collective-permute-done.18 = f32[256,1024]{1,0:T(8,128)S(1)} collective-permute-done((f32[256,1024]{1,0:T(8,128)S(1)}, f32[256,1024]{1,0:T(8,128)S(1)}, u32[]{:S(2)}, u32[]{:S(2)}) %collective-permute-start.18) | collective-permute-done | bytes 1048608 | tf_op jit(solution)/shard_map/ppermute | solution.py:92
  196.6 6.5 %collective-permute-start.9 = (f32[256,512]{1,0:T(8,128)S(1)}, f32[256,512]{1,0:T(8,128)S(1)}, u32[]{:S(2)}, u32[]{:S(2)}) collective-permute-start(f32[256,512]{1,0:T(8,128)S(1)} %get-tuple-element.12), channel_id=1, source_target_pairs={{0,32},{16,48},{32,0},{48,16},{1,33},{17,49},{33,1},{49,17},{2,34}... | collective-permute-start | bytes 1572872 | tf_op jit(solution)/shard_map/ppermute | solution.py:92
  205.6 5.9 %collective-permute-done.10 = f32[256,512]{1,0:T(8,128)S(1)} collective-permute-done((f32[256,512]{1,0:T(8,128)S(1)}, f32[256,512]{1,0:T(8,128)S(1)}, u32[]{:S(2)}, u32[]{:S(2)}) %collective-permute-start.10) | collective-permute-done | bytes 524320 | tf_op jit(solution)/shard_map/ppermute | solution.py:92
  211.4 9.1 %collective-permute-done.9 = f32[256,512]{1,0:T(8,128)S(1)} collective-permute-done((f32[256,512]{1,0:T(8,128)S(1)}, f32[256,512]{1,0:T(8,128)S(1)}, u32[]{:S(2)}, u32[]{:S(2)}) %collective-permute-start.9) | collective-permute-done | bytes 524320 | tf_op jit(solution)/shard_map/ppermute | solution.py:92
  222.9 3.0 %collective-permute-start.22 = (f32[512,16]{0,1:T(8,128)S(1)}, f32[512,16]{0,1:T(8,128)S(1)}, u32[]{:S(2)}, u32[]{:S(2)}) collective-permute-start(f32[512,16]{0,1:T(8,128)S(1)} %multiply_reduce_fusion), channel_id=1, source_target_pairs={{0,16},{16,32},{32,48},{48,0},{1,17},{17,33},{33,49},{49,1},{2,18}... | collective-permute-start | bytes 98312 | tf_op jit(solution)/shard_map/ppermute | solution.py:24
  231.4 4.8 %collective-permute-start.26 = (f32[4,512,16]{1,2,0:T(8,128)S(1)}, f32[4,512,16]{1,2,0:T(8,128)S(1)}, u32[]{:S(2)}, u32[]{:S(2)}) collective-permute-start(f32[4,512,16]{1,2,0:T(8,128)S(1)} %get-tuple-element.20), channel_id=1, source_target_pairs={{0,128},{64,192},{128,0},{192,64},{1,129},{65,193},{129,1},{193,65... | collective-permute-start | bytes 393224 | tf_op jit(solution)/shard_map/ppermute | solution.py:24
  238.1 2.7 %collective-permute-done.26 = f32[4,512,16]{1,2,0:T(8,128)S(1)} collective-permute-done((f32[4,512,16]{1,2,0:T(8,128)S(1)}, f32[4,512,16]{1,2,0:T(8,128)S(1)}, u32[]{:S(2)}, u32[]{:S(2)}) %collective-permute-start.26) | collective-permute-done | bytes 131104 | tf_op jit(solution)/shard_map/ppermute | solution.py:24
  243.3 10.1 %multiply_reduce_fusion.1 = f32[256,512]{1,0:T(8,128)S(1)} fusion(f32[512,16]{0,1:T(8,128)S(1)} %exponential_multiply_fusion, f32[512,16]{0,1:T(8,128)S(1)} %neg.8, f32[512,16]{0,1:T(8,128)S(1)} %copy-done.4, f32[512,16,256]{2,1,0:T(8,128)S(1)} %bitcast.192), kind=kOutput, calls=%fused_computation.4 | convolution fusion | flops 6452871168 | bytes 9011200 | tf_op jit(solution)/shard_map/dot_general | solution.py:132
  (94 shorter events, 55.4 us)
Async XLA Ops:
  6.5 105.7 %all-gather.3.cloned.1.call-start = ((), (), s32[]{:S(2)}) async-start(), calls=%async_computation | async-start | bytes 4718592 | tf_op jit(solution)/shard_map/all_gather | solution.py:67
  6.5 10.4 %collective-permute-start = (bf16[256,512]{1,0:T(8,128)(2,1)}, bf16[256,512]{1,0:T(8,128)(2,1)S(1)}, u32[]{:S(2)}, u32[]{:S(2)}) collective-permute-start(bf16[256,512]{1,0:T(8,128)(2,1)} %param.6), channel_id=1, source_target_pairs={{0,0},{1,16},{2,32},{3,48},{16,1},{17,17},{18,33},{19,49},{32,2},{... | collective-permute-start | bytes 786440 | tf_op jit(solution)/shard_map/ppermute | solution.py:64
  8.1 16.1 %collective-permute-start.1 = (bf16[256,512]{1,0:T(8,128)(2,1)}, bf16[256,512]{1,0:T(8,128)(2,1)S(1)}, u32[]{:S(2)}, u32[]{:S(2)}) collective-permute-start(bf16[256,512]{1,0:T(8,128)(2,1)} %param.6), channel_id=1, source_target_pairs={{0,2},{1,18},{2,34},{3,50},{16,3},{17,19},{18,35},{19,51},{32,0},{... | collective-permute-start | bytes 786440 | tf_op jit(solution)/shard_map/ppermute | solution.py:65
  26.7 30.3 %collective-permute-start.12 = (bf16[512,1024]{1,0:T(8,128)(2,1)S(1)}, bf16[512,1024]{1,0:T(8,128)(2,1)S(1)}, u32[]{:S(2)}, u32[]{:S(2)}) collective-permute-start(bf16[512,1024]{1,0:T(8,128)(2,1)S(1)} %bitcast.194), channel_id=1, source_target_pairs={{0,64},{64,128},{128,192},{1,65},{65,129},{129,193},{2,66},{66,130... | collective-permute-start | bytes 3145736 | tf_op jit(solution)/shard_map/ppermute | solution.py:30
  33.5 28.9 %collective-permute-start.13 = (bf16[512,1024]{1,0:T(8,128)(2,1)S(1)}, bf16[512,1024]{1,0:T(8,128)(2,1)}, u32[]{:S(2)}, u32[]{:S(2)}) collective-permute-start(bf16[512,1024]{1,0:T(8,128)(2,1)S(1)} %bitcast.195), channel_id=1, source_target_pairs={{64,0},{128,64},{192,128},{65,1},{129,65},{193,129},{66,2},{130,66... | collective-permute-start | bytes 3145736 | tf_op jit(solution)/shard_map/ppermute | solution.py:31
  37.3 31.0 %collective-permute-start.2 = (bf16[512,512]{1,0:T(8,128)(2,1)}, bf16[512,512]{1,0:T(8,128)(2,1)}, u32[]{:S(2)}, u32[]{:S(2)}) collective-permute-start(bf16[512,512]{1,0:T(8,128)(2,1)} %slice_bitcast_fusion), channel_id=1, source_target_pairs={{0,64},{64,128},{128,192},{1,65},{65,129},{129,193},{2,66},{66,130... | collective-permute-start | bytes 1572872 | tf_op jit(solution)/shard_map/ppermute | solution.py:30
  41.2 32.3 %collective-permute-start.3 = (bf16[512,512]{1,0:T(8,128)(2,1)}, bf16[512,512]{1,0:T(8,128)(2,1)}, u32[]{:S(2)}, u32[]{:S(2)}) collective-permute-start(bf16[512,512]{1,0:T(8,128)(2,1)} %slice_bitcast_fusion), channel_id=1, source_target_pairs={{64,0},{128,64},{192,128},{65,1},{129,65},{193,129},{66,2},{130,66... | collective-permute-start | bytes 1572872 | tf_op jit(solution)/shard_map/ppermute | solution.py:31
  57.0 51.2 %collective-permute-start.14 = (bf16[512,1024]{1,0:T(8,128)(2,1)S(1)}, bf16[512,1024]{1,0:T(8,128)(2,1)}, u32[]{:S(2)}, u32[]{:S(2)}) collective-permute-start(bf16[512,1024]{1,0:T(8,128)(2,1)S(1)} %collective-permute-done.12), channel_id=1, source_target_pairs={{64,128},{128,192},{65,129},{129,193},{66,130},{130,194},{67,131},... | collective-permute-start | bytes 3145736 | tf_op jit(solution)/shard_map/ppermute | solution.py:35
  62.4 47.6 %collective-permute-start.15 = (bf16[512,1024]{1,0:T(8,128)(2,1)}, bf16[512,1024]{1,0:T(8,128)(2,1)}, u32[]{:S(2)}, u32[]{:S(2)}) collective-permute-start(bf16[512,1024]{1,0:T(8,128)(2,1)} %collective-permute-done.13), channel_id=1, source_target_pairs={{64,0},{128,64},{65,1},{129,65},{66,2},{130,66},{67,3},{131,67},{6... | collective-permute-start | bytes 3145736 | tf_op jit(solution)/shard_map/ppermute | solution.py:36
  68.3 32.8 %collective-permute-start.4 = (bf16[512,512]{1,0:T(8,128)(2,1)}, bf16[512,512]{1,0:T(8,128)(2,1)}, u32[]{:S(2)}, u32[]{:S(2)}) collective-permute-start(bf16[512,512]{1,0:T(8,128)(2,1)} %collective-permute-done.2), channel_id=1, source_target_pairs={{64,128},{128,192},{65,129},{129,193},{66,130},{130,194},{67,131},... | collective-permute-start | bytes 1572872 | tf_op jit(solution)/shard_map/ppermute | solution.py:35
  73.5 31.7 %collective-permute-start.5 = (bf16[512,512]{1,0:T(8,128)(2,1)}, bf16[512,512]{1,0:T(8,128)(2,1)}, u32[]{:S(2)}, u32[]{:S(2)}) collective-permute-start(bf16[512,512]{1,0:T(8,128)(2,1)} %collective-permute-done.3), channel_id=1, source_target_pairs={{64,0},{128,64},{65,1},{129,65},{66,2},{130,66},{67,3},{131,67},{6... | collective-permute-start | bytes 1572872 | tf_op jit(solution)/shard_map/ppermute | solution.py:36
  101.1 60.6 %collective-permute-start.6 = (bf16[512,512]{1,0:T(8,128)(2,1)}, bf16[512,512]{1,0:T(8,128)(2,1)}, u32[]{:S(2)}, u32[]{:S(2)}) collective-permute-start(bf16[512,512]{1,0:T(8,128)(2,1)} %collective-permute-done.4), channel_id=1, source_target_pairs={{128,192},{129,193},{130,194},{131,195},{132,196},{133,197},{134,1... | collective-permute-start | bytes 1572872 | tf_op jit(solution)/shard_map/ppermute | solution.py:35
  105.2 56.5 %collective-permute-start.7 = (bf16[512,512]{1,0:T(8,128)(2,1)}, bf16[512,512]{1,0:T(8,128)(2,1)}, u32[]{:S(2)}, u32[]{:S(2)}) collective-permute-start(bf16[512,512]{1,0:T(8,128)(2,1)} %collective-permute-done.5), channel_id=1, source_target_pairs={{64,0},{65,1},{66,2},{67,3},{68,4},{69,5},{70,6},{71,7},{72,8},{73... | collective-permute-start | bytes 1572872 | tf_op jit(solution)/shard_map/ppermute | solution.py:36
  108.2 14.7 %collective-permute-start.16 = (bf16[512,1024]{1,0:T(8,128)(2,1)}, bf16[512,1024]{1,0:T(8,128)(2,1)}, u32[]{:S(2)}, u32[]{:S(2)}) collective-permute-start(bf16[512,1024]{1,0:T(8,128)(2,1)} %collective-permute-done.14), channel_id=1, source_target_pairs={{128,192},{129,193},{130,194},{131,195},{132,196},{133,197},{134,1... | collective-permute-start | bytes 3145736 | tf_op jit(solution)/shard_map/ppermute | solution.py:35
  110.0 30.7 %collective-permute-start.17 = (bf16[512,1024]{1,0:T(8,128)(2,1)}, bf16[512,1024]{1,0:T(8,128)(2,1)}, u32[]{:S(2)}, u32[]{:S(2)}) collective-permute-start(bf16[512,1024]{1,0:T(8,128)(2,1)} %collective-permute-done.15), channel_id=1, source_target_pairs={{64,0},{65,1},{66,2},{67,3},{68,4},{69,5},{70,6},{71,7},{72,8},{73... | collective-permute-start | bytes 3145736 | tf_op jit(solution)/shard_map/ppermute | solution.py:36
  144.8 51.9 %collective-permute-start.18 = (f32[256,1024]{1,0:T(8,128)S(1)}, f32[256,1024]{1,0:T(8,128)S(1)}, u32[]{:S(2)}, u32[]{:S(2)}) collective-permute-start(f32[256,1024]{1,0:T(8,128)S(1)} %get-tuple-element.7), channel_id=1, source_target_pairs={{0,16},{16,32},{32,48},{48,0},{1,17},{17,33},{33,49},{49,1},{2,18}... | collective-permute-start | bytes 3145736 | tf_op jit(solution)/shard_map/ppermute | solution.py:92
  145.0 58.1 %collective-permute-start.19 = (f32[256,1024]{1,0:T(8,128)S(1)}, f32[256,1024]{1,0:T(8,128)S(1)}, u32[]{:S(2)}, u32[]{:S(2)}) collective-permute-start(f32[256,1024]{1,0:T(8,128)S(1)} %get-tuple-element.9), channel_id=1, source_target_pairs={{0,32},{16,48},{32,0},{48,16},{1,33},{17,49},{33,1},{49,17},{2,34}... | collective-permute-start | bytes 3145736 | tf_op jit(solution)/shard_map/ppermute | solution.py:92
  154.0 49.1 %collective-permute-start.20 = (f32[256,1024]{1,0:T(8,128)S(1)}, f32[256,1024]{1,0:T(8,128)S(1)}, u32[]{:S(2)}, u32[]{:S(2)}) collective-permute-start(f32[256,1024]{1,0:T(8,128)S(1)} %get-tuple-element.8), channel_id=1, source_target_pairs={{0,48},{16,0},{32,16},{48,32},{1,49},{17,1},{33,17},{49,33},{2,50}... | collective-permute-start | bytes 3145736 | tf_op jit(solution)/shard_map/ppermute | solution.py:92
  164.1 47.4 %collective-permute-start.10 = (f32[256,512]{1,0:T(8,128)S(1)}, f32[256,512]{1,0:T(8,128)S(1)}, u32[]{:S(2)}, u32[]{:S(2)}) collective-permute-start(f32[256,512]{1,0:T(8,128)S(1)} %get-tuple-element.11), channel_id=1, source_target_pairs={{0,48},{16,0},{32,16},{48,32},{1,49},{17,1},{33,17},{49,33},{2,50}... | collective-permute-start | bytes 1572872 | tf_op jit(solution)/shard_map/ppermute | solution.py:92
  164.2 47.3 %collective-permute-start.8 = (f32[256,512]{1,0:T(8,128)S(1)}, f32[256,512]{1,0:T(8,128)S(1)}, u32[]{:S(2)}, u32[]{:S(2)}) collective-permute-start(f32[256,512]{1,0:T(8,128)S(1)} %get-tuple-element.10), channel_id=1, source_target_pairs={{0,16},{16,32},{32,48},{48,0},{1,17},{17,33},{33,49},{49,1},{2,18}... | collective-permute-start | bytes 1572872 | tf_op jit(solution)/shard_map/ppermute | solution.py:92
  196.6 23.9 %collective-permute-start.9 = (f32[256,512]{1,0:T(8,128)S(1)}, f32[256,512]{1,0:T(8,128)S(1)}, u32[]{:S(2)}, u32[]{:S(2)}) collective-permute-start(f32[256,512]{1,0:T(8,128)S(1)} %get-tuple-element.12), channel_id=1, source_target_pairs={{0,32},{16,48},{32,0},{48,16},{1,33},{17,49},{33,1},{49,17},{2,34}... | collective-permute-start | bytes 1572872 | tf_op jit(solution)/shard_map/ppermute | solution.py:92
  203.6 17.1 %collective-permute-start.21 = (bf16[2,2,512]{2,0,1:T(2,128)(2,1)S(1)}, bf16[2,2,512]{2,0,1:T(2,128)(2,1)S(1)}, u32[]{:S(2)}, u32[]{:S(2)}) collective-permute-start(bf16[2,2,512]{2,0,1:T(2,128)(2,1)S(1)} %pad_maximum_fusion.2), channel_id=1, source_target_pairs={{0,16},{16,32},{32,48},{48,64},{64,80},{80,96},{96,112},{112,128},... | collective-permute-start | bytes 12296 | tf_op jit(solution)/shard_map/ppermute | solution.py:16
  228.6 7.9 %collective-permute-start.11 = (bf16[2,1,512]{2,0,1:T(2,128)(2,1)S(1)}, bf16[2,1,512]{2,0,1:T(2,128)(2,1)S(1)}, u32[]{:S(2)}, u32[]{:S(2)}) collective-permute-start(bf16[2,1,512]{2,0,1:T(2,128)(2,1)S(1)} %slice_bitcast_fusion.6), channel_id=1, source_target_pairs={{0,16},{16,32},{32,48},{48,64},{64,80},{80,96},{96,112},{112,128},... | collective-permute-start | bytes 6152 | tf_op jit(solution)/shard_map/ppermute | solution.py:16
  231.4 9.4 %collective-permute-start.26 = (f32[4,512,16]{1,2,0:T(8,128)S(1)}, f32[4,512,16]{1,2,0:T(8,128)S(1)}, u32[]{:S(2)}, u32[]{:S(2)}) collective-permute-start(f32[4,512,16]{1,2,0:T(8,128)S(1)} %get-tuple-element.20), channel_id=1, source_target_pairs={{0,128},{64,192},{128,0},{192,64},{1,129},{65,193},{129,1},{193,65... | collective-permute-start | bytes 393224 | tf_op jit(solution)/shard_map/ppermute | solution.py:24
  (10 other events, 130.1 us)
Sparse Core Ops, SparseCore 0:
  25.3 40.9 all-gather.2

commit v2 on v0

--- a/solution.py
+++ b/solution.py
@@ -62,13 +62,22 @@
     ]
     near = lax.ppermute(tokens, ("x",) + SUB, swap)
     far = lax.ppermute(tokens, ("x",) + SUB, cross)
-    both = jnp.stack([jnp.where(me_h == 0, near, far), jnp.where(me_h == 0, far, near)])
-    gathered = lax.all_gather(both, ("y", "c"), axis=0, tiled=False)
-    blocks = gathered.reshape(-1, pair, halves, tok_rows, feat_block)
+    near_all = lax.all_gather(near, ("y", "c"), axis=0, tiled=False)
+    far_all = lax.all_gather(far, ("y", "c"), axis=0, tiled=False)
+    near_blocks = near_all.reshape(-1, pair, tok_rows, feat_block)
+    far_blocks = far_all.reshape(-1, pair, tok_rows, feat_block)
 
     def contribution(source, weight):
-        taken = lax.dynamic_index_in_dim(blocks, source, axis=0, keepdims=False)
-        return jnp.einsum("chru,uk->hcrk", taken, weight, preferred_element_type=jnp.float32)
+        parts = []
+        for copy in (near_blocks, far_blocks):
+            taken = lax.dynamic_index_in_dim(copy, source, axis=0, keepdims=False)
+            parts.append(
+                jnp.einsum("cru,uk->crk", taken, weight, preferred_element_type=jnp.float32)
+            )
+        own_half, other_half = parts
+        low_half = jnp.where(me_h == 0, own_half, other_half)
+        high_half = jnp.where(me_h == 0, other_half, own_half)
+        return jnp.stack([low_half, high_half])
 
     reduced = {}
     for s in order:
@@ -131,10 +140,8 @@
         tok_rows, width_local, mode_count
     )
     shrink = jnp.exp(-decay_rate[None, :, :] * position[:, None, None])
-    weighted = residue[None] * shrink
-    inside = jnp.sum(weighted * running_sum, axis=2)
     entering = (incoming * jnp.exp(-decay_rate))[None]
-    convolved = inside + jnp.sum(weighted * entering, axis=2)
+    convolved = jnp.sum(residue[None] * shrink * (running_sum + entering), axis=2)
     long_mix = convolved + skip_gain[None, :] * gated_wide
     query_gate = short_conv(order[-1:])[:, 0]
     return (query_gate * long_mix).astype(jnp.bfloat16)

time: 248 us -> 266 us (1.073)
  waiting for transfers between devices: 111 us -> 119 us
  local copies, waits for them, and re-layouts: 2.63 us -> 7.23 us
    ppermute x3, waiting for transfers between devices: 0.66 us -> 20.4 us  [line_gather(): near_a = lax.ppermute(piece, axis, [(i + 1, i) for i in range(size - 1)])]
    ppermute x6, waiting for transfers between devices: 0.79 us -> 19.4 us  [line_gather(): lax.ppermute(near_b, axis, [(i, i + 1) for i in range(d - 1, size - 1)])]
    ppermute x6, waiting for transfers between devices: 33 us -> 14.8 us  [line_gather(): lax.ppermute(near_a, axis, [(i + 1, i) for i in range(0, size - d)])]
    ppermute x9, starting transfers between devices: 14.9 us -> 22.5 us  [block(): total = total + lax.ppermute(piece, 'x', route)]
    ppermute x6, starting transfers between devices: 4.94 us -> 12.4 us  [ring_sends(): received.append(lax.ppermute(pieces(k, position), axis, route))]
    ppermute x9, waiting for transfers between devices: 39.7 us -> 33.6 us  [block(): total = total + lax.ppermute(piece, 'x', route)]
    ppermute x3, starting transfers between devices: 14.6 us -> 8.68 us  [line_gather(): near_b = lax.ppermute(piece, axis, [(i, i + 1) for i in range(size - 1)])]
    ppermute x2, waiting for transfers between devices: 5.6 us -> 0.01 us  [from_behind(): return lax.ppermute(block, axis, route)]
  transfers between devices with their start and end apart: 38 -> 39, of which waited for: 19 -> 14; matrix products, arithmetic and copies ran while one was open for 12% -> 10% of each run, Pallas kernels for 0% -> 0%
where the time goes in v2:
time: 266 us; the launch traced here: 264 us
  waiting for transfers between devices  119 us (45%)
  starting transfers between devices  86.1 us (32%)
  matrix products  28 us (11%)
  between operations  14.3 us (5%)
  other arithmetic  9.45 us (4%)
  local copies, waits for them, and re-layouts  7.23 us (3%)
    ppermute x9, waiting for transfers between devices, block(): total = total + lax.ppermute(piece, 'x', route)  33.6 us
    ppermute x9, starting transfers between devices, block(): total = total + lax.ppermute(piece, 'x', route)  22.5 us
    ppermute x3, waiting for transfers between devices, line_gather(): near_a = lax.ppermute(piece, axis, [(i + 1, i) for i in range(size - 1)])  20.4 us
    ppermute x6, waiting for transfers between devices, line_gather(): lax.ppermute(near_b, axis, [(i, i + 1) for i in range(d - 1, size - 1)])  19.4 us
    dot_general x30, matrix products, contribution(): jnp.einsum('cru,uk->crk', taken, weight, preferred_element_type=jnp.float32)  18 us
    all_gather x1, waiting for transfers between devices, block(): near_all = lax.all_gather(near, ('y', 'c'), axis=0, tiled=False)  15.2 us
    ppermute x6, waiting for transfers between devices, line_gather(): lax.ppermute(near_a, axis, [(i + 1, i) for i in range(0, size - d)])  14.8 us
    ppermute x6, starting transfers between devices, ring_sends(): received.append(lax.ppermute(pieces(k, position), axis, route))  12.4 us
  transfers between devices with their start and end apart: 39, of which 14 were waited for; matrix products, arithmetic and copies ran while one was open for 10% of the time, Pallas kernels for 0%

profile of v2, /device:TPU:32, one launch (start us, length us, event | category | flops | bytes accessed | tf_op | source)
XLA Modules:
  0.0 264.0 jit_solution(1669871663303640808)
XLA Ops:
  6.5 6.3 %collective-permute-start.1 = (bf16[256,512]{1,0:T(8,128)(2,1)}, bf16[256,512]{1,0:T(8,128)(2,1)S(1)}, u32[]{:S(2)}, u32[]{:S(2)}) collective-permute-start(bf16[256,512]{1,0:T(8,128)(2,1)} %param.6), channel_id=1, source_target_pairs={{0,2},{1,18},{2,34},{3,50},{16,3},{17,19},{18,35},{19,51},{32,0},{... | collective-permute-start | bytes 786440 | tf_op jit(solution)/shard_map/ppermute | solution.py:64
  12.8 12.3 %collective-permute-done.1 = bf16[256,512]{1,0:T(8,128)(2,1)S(1)} collective-permute-done((bf16[256,512]{1,0:T(8,128)(2,1)}, bf16[256,512]{1,0:T(8,128)(2,1)S(1)}, u32[]{:S(2)}, u32[]{:S(2)}) %collective-permute-start.1) | collective-permute-done | bytes 262176 | tf_op jit(solution)/shard_map/ppermute | solution.py:64
  30.8 2.9 %collective-permute-start.21 = (bf16[512,512]{1,0:T(8,128)(2,1)}, bf16[512,512]{1,0:T(8,128)(2,1)S(1)}, u32[]{:S(2)}, u32[]{:S(2)}) collective-permute-start(bf16[512,512]{1,0:T(8,128)(2,1)} %get-tuple-element.48), channel_id=1, source_target_pairs={{0,64},{64,128},{128,192},{1,65},{65,129},{129,193},{2,66},{66,130... | collective-permute-start | bytes 1572872 | tf_op jit(solution)/shard_map/ppermute | solution.py:30
  33.8 2.9 %collective-permute-start.22 = (bf16[512,512]{1,0:T(8,128)(2,1)}, bf16[512,512]{1,0:T(8,128)(2,1)S(1)}, u32[]{:S(2)}, u32[]{:S(2)}) collective-permute-start(bf16[512,512]{1,0:T(8,128)(2,1)} %get-tuple-element.48), channel_id=1, source_target_pairs={{64,0},{128,64},{192,128},{65,1},{129,65},{193,129},{66,2},{130,66... | collective-permute-start | bytes 1572872 | tf_op jit(solution)/shard_map/ppermute | solution.py:31
  36.7 2.9 %collective-permute-start.12 = (bf16[512,512]{1,0:T(8,128)(2,1)}, bf16[512,512]{1,0:T(8,128)(2,1)S(1)}, u32[]{:S(2)}, u32[]{:S(2)}) collective-permute-start(bf16[512,512]{1,0:T(8,128)(2,1)} %get-tuple-element.46), channel_id=1, source_target_pairs={{0,64},{64,128},{128,192},{1,65},{65,129},{129,193},{2,66},{66,130... | collective-permute-start | bytes 1572872 | tf_op jit(solution)/shard_map/ppermute | solution.py:30
  39.6 3.0 %collective-permute-start.13 = (bf16[512,512]{1,0:T(8,128)(2,1)}, bf16[512,512]{1,0:T(8,128)(2,1)S(1)}, u32[]{:S(2)}, u32[]{:S(2)}) collective-permute-start(bf16[512,512]{1,0:T(8,128)(2,1)} %get-tuple-element.46), channel_id=1, source_target_pairs={{64,0},{128,64},{192,128},{65,1},{129,65},{193,129},{66,2},{130,66... | collective-permute-start | bytes 1572872 | tf_op jit(solution)/shard_map/ppermute | solution.py:31
  42.6 2.9 %collective-permute-start.2 = (bf16[512,512]{1,0:T(8,128)(2,1)}, bf16[512,512]{1,0:T(8,128)(2,1)S(1)}, u32[]{:S(2)}, u32[]{:S(2)}) collective-permute-start(bf16[512,512]{1,0:T(8,128)(2,1)} %get-tuple-element.47), channel_id=1, source_target_pairs={{0,64},{64,128},{128,192},{1,65},{65,129},{129,193},{2,66},{66,130... | collective-permute-start | bytes 1572872 | tf_op jit(solution)/shard_map/ppermute | solution.py:30
  45.7 20.4 %collective-permute-done.13 = bf16[512,512]{1,0:T(8,128)(2,1)S(1)} collective-permute-done((bf16[512,512]{1,0:T(8,128)(2,1)}, bf16[512,512]{1,0:T(8,128)(2,1)S(1)}, u32[]{:S(2)}, u32[]{:S(2)}) %collective-permute-start.13) | collective-permute-done | bytes 524320 | tf_op jit(solution)/shard_map/ppermute | solution.py:31
  69.8 15.2 %all-gather.5.cloned.1.call-done = bf16[2048,512]{1,0:T(8,128)(2,1)} async-done(((bf16[256,512]{1,0:T(8,128)(2,1)}), bf16[2048,512]{1,0:T(8,128)(2,1)}) %all-gather.5.cloned.1.call-update) | async-done | bytes 2097168 | tf_op jit(solution)/shard_map/all_gather | solution.py:65
  92.4 3.5 %collective-permute-start.23 = (bf16[512,512]{1,0:T(8,128)(2,1)S(1)}, bf16[512,512]{1,0:T(8,128)(2,1)S(1)}, u32[]{:S(2)}, u32[]{:S(2)}) collective-permute-start(bf16[512,512]{1,0:T(8,128)(2,1)S(1)} %collective-permute-done.21), channel_id=1, source_target_pairs={{64,128},{128,192},{65,129},{129,193},{66,130},{130,194},{67,131},... | collective-permute-start | bytes 1572872 | tf_op jit(solution)/shard_map/ppermute | solution.py:35
  100.6 4.0 %collective-permute-start.4 = (bf16[512,512]{1,0:T(8,128)(2,1)S(1)}, bf16[512,512]{1,0:T(8,128)(2,1)S(1)}, u32[]{:S(2)}, u32[]{:S(2)}) collective-permute-start(bf16[512,512]{1,0:T(8,128)(2,1)S(1)} %collective-permute-done.2), channel_id=1, source_target_pairs={{64,128},{128,192},{65,129},{129,193},{66,130},{130,194},{67,131},... | collective-permute-start | bytes 1572872 | tf_op jit(solution)/shard_map/ppermute | solution.py:35
  104.6 3.5 %collective-permute-done.23 = bf16[512,512]{1,0:T(8,128)(2,1)S(1)} collective-permute-done((bf16[512,512]{1,0:T(8,128)(2,1)S(1)}, bf16[512,512]{1,0:T(8,128)(2,1)S(1)}, u32[]{:S(2)}, u32[]{:S(2)}) %collective-permute-start.23) | collective-permute-done | bytes 524320 | tf_op jit(solution)/shard_map/ppermute | solution.py:35
  110.1 9.3 %collective-permute-done.14 = bf16[512,512]{1,0:T(8,128)(2,1)S(1)} collective-permute-done((bf16[512,512]{1,0:T(8,128)(2,1)S(1)}, bf16[512,512]{1,0:T(8,128)(2,1)S(1)}, u32[]{:S(2)}, u32[]{:S(2)}) %collective-permute-start.14) | collective-permute-done | bytes 524320 | tf_op jit(solution)/shard_map/ppermute | solution.py:35
  123.0 6.6 %collective-permute-done.4 = bf16[512,512]{1,0:T(8,128)(2,1)S(1)} collective-permute-done((bf16[512,512]{1,0:T(8,128)(2,1)S(1)}, bf16[512,512]{1,0:T(8,128)(2,1)S(1)}, u32[]{:S(2)}, u32[]{:S(2)}) %collective-permute-start.4) | collective-permute-done | bytes 524320 | tf_op jit(solution)/shard_map/ppermute | solution.py:35
  133.0 5.4 %collective-permute-done.17 = bf16[512,512]{1,0:T(8,128)(2,1)S(1)} collective-permute-done((bf16[512,512]{1,0:T(8,128)(2,1)S(1)}, bf16[512,512]{1,0:T(8,128)(2,1)S(1)}, u32[]{:S(2)}, u32[]{:S(2)}) %collective-permute-start.17) | collective-permute-done | bytes 524320 | tf_op jit(solution)/shard_map/ppermute | solution.py:36
  140.1 9.4 %collective-permute-done.26 = bf16[512,512]{1,0:T(8,128)(2,1)S(1)} collective-permute-done((bf16[512,512]{1,0:T(8,128)(2,1)S(1)}, bf16[512,512]{1,0:T(8,128)(2,1)S(1)}, u32[]{:S(2)}, u32[]{:S(2)}) %collective-permute-start.26) | collective-permute-done | bytes 524320 | tf_op jit(solution)/shard_map/ppermute | solution.py:36
  173.5 6.9 %collective-permute-done.19 = f32[256,512]{1,0:T(8,128)S(1)} collective-permute-done((f32[256,512]{1,0:T(8,128)S(1)}, f32[256,512]{1,0:T(8,128)S(1)}, u32[]{:S(2)}, u32[]{:S(2)}) %collective-permute-start.19) | collective-permute-done | bytes 524320 | tf_op jit(solution)/shard_map/ppermute | solution.py:100
  182.7 9.0 %collective-permute-done.27 = f32[256,512]{1,0:T(8,128)S(1)} collective-permute-done((f32[256,512]{1,0:T(8,128)S(1)}, f32[256,512]{1,0:T(8,128)S(1)}, u32[]{:S(2)}, u32[]{:S(2)}) %collective-permute-start.27) | collective-permute-done | bytes 524320 | tf_op jit(solution)/shard_map/ppermute | solution.py:100
  191.6 11.0 %collective-permute-start.9 = (f32[256,512]{1,0:T(8,128)S(1)}, f32[256,512]{1,0:T(8,128)S(1)}, u32[]{:S(2)}, u32[]{:S(2)}) collective-permute-start(f32[256,512]{1,0:T(8,128)S(1)} %get-tuple-element.35), channel_id=1, source_target_pairs={{0,32},{16,48},{32,0},{48,16},{1,33},{17,49},{33,1},{49,17},{2,34}... | collective-permute-start | bytes 1572872 | tf_op jit(solution)/shard_map/ppermute | solution.py:100
  205.3 8.7 %collective-permute-done.10 = f32[256,512]{1,0:T(8,128)S(1)} collective-permute-done((f32[256,512]{1,0:T(8,128)S(1)}, f32[256,512]{1,0:T(8,128)S(1)}, u32[]{:S(2)}, u32[]{:S(2)}) %collective-permute-start.10) | collective-permute-done | bytes 524320 | tf_op jit(solution)/shard_map/ppermute | solution.py:100
  214.0 9.0 %collective-permute-done.9 = f32[256,512]{1,0:T(8,128)S(1)} collective-permute-done((f32[256,512]{1,0:T(8,128)S(1)}, f32[256,512]{1,0:T(8,128)S(1)}, u32[]{:S(2)}, u32[]{:S(2)}) %collective-permute-start.9) | collective-permute-done | bytes 524320 | tf_op jit(solution)/shard_map/ppermute | solution.py:100
  230.3 2.9 %collective-permute-start.11 = (bf16[2,1,512]{2,0,1:T(2,128)(2,1)S(1)}, bf16[2,1,512]{2,0,1:T(2,128)(2,1)S(1)}, u32[]{:S(2)}, u32[]{:S(2)}) collective-permute-start(bf16[2,1,512]{2,0,1:T(2,128)(2,1)S(1)} %slice_bitcast_fusion.6), channel_id=1, source_target_pairs={{0,16},{16,32},{32,48},{48,64},{64,80},{80,96},{96,112},{112,128},... | collective-permute-start | bytes 6152 | tf_op jit(solution)/shard_map/ppermute | solution.py:16
  233.2 5.5 %collective-permute-start.35 = (f32[4,512,16]{1,2,0:T(8,128)S(1)}, f32[4,512,16]{1,2,0:T(8,128)S(1)}, u32[]{:S(2)}, u32[]{:S(2)}) collective-permute-start(f32[4,512,16]{1,2,0:T(8,128)S(1)} %get-tuple-element.50), channel_id=1, source_target_pairs={{0,128},{64,192},{128,0},{192,64},{1,129},{65,193},{129,1},{193,65... | collective-permute-start | bytes 393224 | tf_op jit(solution)/shard_map/ppermute | solution.py:24
  246.1 10.1 %multiply_reduce_fusion.1 = f32[256,512]{1,0:T(8,128)S(1)} fusion(f32[512,16]{0,1:T(8,128)S(1)} %exponential_multiply_fusion, f32[512,16]{0,1:T(8,128)S(1)} %neg.8, f32[512,16]{0,1:T(8,128)S(1)} %copy-done.10, f32[512,16,256]{2,1,0:T(8,128)S(1)} %bitcast.396), kind=kOutput, calls=%fused_computation.4 | convolution fusion | flops 6452871168 | bytes 9011200 | tf_op jit(solution)/shard_map/dot_general | solution.py:139
  (143 shorter events, 76.2 us)
Async XLA Ops:
  6.5 61.5 %all-gather.7.cloned.1.call-start = ((), (), s32[]{:S(2)}) async-start(), calls=%async_computation.1 | async-start | bytes 2359296 | tf_op jit(solution)/shard_map/all_gather | solution.py:66
  25.8 59.1 %all-gather.5.cloned.1.call-start = ((), (), s32[]{:S(2)}) async-start(), calls=%async_computation | async-start | bytes 2359296 | tf_op jit(solution)/shard_map/all_gather | solution.py:65
  30.8 58.5 %collective-permute-start.21 = (bf16[512,512]{1,0:T(8,128)(2,1)}, bf16[512,512]{1,0:T(8,128)(2,1)S(1)}, u32[]{:S(2)}, u32[]{:S(2)}) collective-permute-start(bf16[512,512]{1,0:T(8,128)(2,1)} %get-tuple-element.48), channel_id=1, source_target_pairs={{0,64},{64,128},{128,192},{1,65},{65,129},{129,193},{2,66},{66,130... | collective-permute-start | bytes 1572872 | tf_op jit(solution)/shard_map/ppermute | solution.py:30
  33.8 58.6 %collective-permute-start.22 = (bf16[512,512]{1,0:T(8,128)(2,1)}, bf16[512,512]{1,0:T(8,128)(2,1)S(1)}, u32[]{:S(2)}, u32[]{:S(2)}) collective-permute-start(bf16[512,512]{1,0:T(8,128)(2,1)} %get-tuple-element.48), channel_id=1, source_target_pairs={{64,0},{128,64},{192,128},{65,1},{129,65},{193,129},{66,2},{130,66... | collective-permute-start | bytes 1572872 | tf_op jit(solution)/shard_map/ppermute | solution.py:31
  36.7 59.2 %collective-permute-start.12 = (bf16[512,512]{1,0:T(8,128)(2,1)}, bf16[512,512]{1,0:T(8,128)(2,1)S(1)}, u32[]{:S(2)}, u32[]{:S(2)}) collective-permute-start(bf16[512,512]{1,0:T(8,128)(2,1)} %get-tuple-element.46), channel_id=1, source_target_pairs={{0,64},{64,128},{128,192},{1,65},{65,129},{129,193},{2,66},{66,130... | collective-permute-start | bytes 1572872 | tf_op jit(solution)/shard_map/ppermute | solution.py:30
  39.6 26.5 %collective-permute-start.13 = (bf16[512,512]{1,0:T(8,128)(2,1)}, bf16[512,512]{1,0:T(8,128)(2,1)S(1)}, u32[]{:S(2)}, u32[]{:S(2)}) collective-permute-start(bf16[512,512]{1,0:T(8,128)(2,1)} %get-tuple-element.46), channel_id=1, source_target_pairs={{64,0},{128,64},{192,128},{65,1},{129,65},{193,129},{66,2},{130,66... | collective-permute-start | bytes 1572872 | tf_op jit(solution)/shard_map/ppermute | solution.py:31
  42.6 56.1 %collective-permute-start.2 = (bf16[512,512]{1,0:T(8,128)(2,1)}, bf16[512,512]{1,0:T(8,128)(2,1)S(1)}, u32[]{:S(2)}, u32[]{:S(2)}) collective-permute-start(bf16[512,512]{1,0:T(8,128)(2,1)} %get-tuple-element.47), channel_id=1, source_target_pairs={{0,64},{64,128},{128,192},{1,65},{65,129},{129,193},{2,66},{66,130... | collective-permute-start | bytes 1572872 | tf_op jit(solution)/shard_map/ppermute | solution.py:30
  66.1 34.5 %collective-permute-start.3 = (bf16[512,512]{1,0:T(8,128)(2,1)}, bf16[512,512]{1,0:T(8,128)(2,1)}, u32[]{:S(2)}, u32[]{:S(2)}) collective-permute-start(bf16[512,512]{1,0:T(8,128)(2,1)} %get-tuple-element.47), channel_id=1, source_target_pairs={{64,0},{128,64},{192,128},{65,1},{129,65},{193,129},{66,2},{130,66... | collective-permute-start | bytes 1572872 | tf_op jit(solution)/shard_map/ppermute | solution.py:31
  90.0 30.1 %collective-permute-start.15 = (bf16[512,512]{1,0:T(8,128)(2,1)S(1)}, bf16[512,512]{1,0:T(8,128)(2,1)S(1)}, u32[]{:S(2)}, u32[]{:S(2)}) collective-permute-start(bf16[512,512]{1,0:T(8,128)(2,1)S(1)} %copy-done.4), channel_id=1, source_target_pairs={{64,0},{128,64},{65,1},{129,65},{66,2},{130,66},{67,3},{131,67},{6... | collective-permute-start | bytes 1572872 | tf_op jit(solution)/shard_map/ppermute | solution.py:36
  95.9 23.5 %collective-permute-start.14 = (bf16[512,512]{1,0:T(8,128)(2,1)S(1)}, bf16[512,512]{1,0:T(8,128)(2,1)S(1)}, u32[]{:S(2)}, u32[]{:S(2)}) collective-permute-start(bf16[512,512]{1,0:T(8,128)(2,1)S(1)} %collective-permute-done.12), channel_id=1, source_target_pairs={{64,128},{128,192},{65,129},{129,193},{66,130},{130,194},{67,131},... | collective-permute-start | bytes 1572872 | tf_op jit(solution)/shard_map/ppermute | solution.py:35
  98.7 23.6 %collective-permute-start.24 = (bf16[512,512]{1,0:T(8,128)(2,1)S(1)}, bf16[512,512]{1,0:T(8,128)(2,1)S(1)}, u32[]{:S(2)}, u32[]{:S(2)}) collective-permute-start(bf16[512,512]{1,0:T(8,128)(2,1)S(1)} %collective-permute-done.22), channel_id=1, source_target_pairs={{64,0},{128,64},{65,1},{129,65},{66,2},{130,66},{67,3},{131,67},{6... | collective-permute-start | bytes 1572872 | tf_op jit(solution)/shard_map/ppermute | solution.py:36
  100.6 29.0 %collective-permute-start.4 = (bf16[512,512]{1,0:T(8,128)(2,1)S(1)}, bf16[512,512]{1,0:T(8,128)(2,1)S(1)}, u32[]{:S(2)}, u32[]{:S(2)}) collective-permute-start(bf16[512,512]{1,0:T(8,128)(2,1)S(1)} %collective-permute-done.2), channel_id=1, source_target_pairs={{64,128},{128,192},{65,129},{129,193},{66,130},{130,194},{67,131},... | collective-permute-start | bytes 1572872 | tf_op jit(solution)/shard_map/ppermute | solution.py:35
  108.1 22.8 %collective-permute-start.5 = (bf16[512,512]{1,0:T(8,128)(2,1)}, bf16[512,512]{1,0:T(8,128)(2,1)S(1)}, u32[]{:S(2)}, u32[]{:S(2)}) collective-permute-start(bf16[512,512]{1,0:T(8,128)(2,1)} %collective-permute-done.3), channel_id=1, source_target_pairs={{64,0},{128,64},{65,1},{129,65},{66,2},{130,66},{67,3},{131,67},{6... | collective-permute-start | bytes 1572872 | tf_op jit(solution)/shard_map/ppermute | solution.py:36
  130.9 33.8 %collective-permute-start.6 = (bf16[512,512]{1,0:T(8,128)(2,1)S(1)}, bf16[512,512]{1,0:T(8,128)(2,1)S(1)}, u32[]{:S(2)}, u32[]{:S(2)}) collective-permute-start(bf16[512,512]{1,0:T(8,128)(2,1)S(1)} %collective-permute-done.4), channel_id=1, source_target_pairs={{128,192},{129,193},{130,194},{131,195},{132,196},{133,197},{134,1... | collective-permute-start | bytes 1572872 | tf_op jit(solution)/shard_map/ppermute | solution.py:35
  131.6 33.8 %collective-permute-start.7 = (bf16[512,512]{1,0:T(8,128)(2,1)S(1)}, bf16[512,512]{1,0:T(8,128)(2,1)S(1)}, u32[]{:S(2)}, u32[]{:S(2)}) collective-permute-start(bf16[512,512]{1,0:T(8,128)(2,1)S(1)} %collective-permute-done.5), channel_id=1, source_target_pairs={{64,0},{65,1},{66,2},{67,3},{68,4},{69,5},{70,6},{71,7},{72,8},{73... | collective-permute-start | bytes 1572872 | tf_op jit(solution)/shard_map/ppermute | solution.py:36
  153.6 26.7 %collective-permute-start.19 = (f32[256,512]{1,0:T(8,128)S(1)}, f32[256,512]{1,0:T(8,128)S(1)}, u32[]{:S(2)}, u32[]{:S(2)}) collective-permute-start(f32[256,512]{1,0:T(8,128)S(1)} %get-tuple-element.9), channel_id=1, source_target_pairs={{0,32},{16,48},{32,0},{48,16},{1,33},{17,49},{33,1},{49,17},{2,34}... | collective-permute-start | bytes 1572872 | tf_op jit(solution)/shard_map/ppermute | solution.py:100
  156.3 26.0 %collective-permute-start.20 = (f32[256,512]{1,0:T(8,128)S(1)}, f32[256,512]{1,0:T(8,128)S(1)}, u32[]{:S(2)}, u32[]{:S(2)}) collective-permute-start(f32[256,512]{1,0:T(8,128)S(1)} %get-tuple-element.8), channel_id=1, source_target_pairs={{0,48},{16,0},{32,16},{48,32},{1,49},{17,1},{33,17},{49,33},{2,50}... | collective-permute-start | bytes 1572872 | tf_op jit(solution)/shard_map/ppermute | solution.py:100
  164.8 26.9 %collective-permute-start.27 = (f32[256,512]{1,0:T(8,128)S(1)}, f32[256,512]{1,0:T(8,128)S(1)}, u32[]{:S(2)}, u32[]{:S(2)}) collective-permute-start(f32[256,512]{1,0:T(8,128)S(1)} %get-tuple-element.20), channel_id=1, source_target_pairs={{0,16},{16,32},{32,48},{48,0},{1,17},{17,33},{33,49},{49,1},{2,18}... | collective-permute-start | bytes 1572872 | tf_op jit(solution)/shard_map/ppermute | solution.py:100
  165.4 37.5 %collective-permute-start.28 = (f32[256,512]{1,0:T(8,128)S(1)}, f32[256,512]{1,0:T(8,128)S(1)}, u32[]{:S(2)}, u32[]{:S(2)}) collective-permute-start(f32[256,512]{1,0:T(8,128)S(1)} %get-tuple-element.22), channel_id=1, source_target_pairs={{0,32},{16,48},{32,0},{48,16},{1,33},{17,49},{33,1},{49,17},{2,34}... | collective-permute-start | bytes 1572872 | tf_op jit(solution)/shard_map/ppermute | solution.py:100
  170.1 32.8 %collective-permute-start.29 = (f32[256,512]{1,0:T(8,128)S(1)}, f32[256,512]{1,0:T(8,128)S(1)}, u32[]{:S(2)}, u32[]{:S(2)}) collective-permute-start(f32[256,512]{1,0:T(8,128)S(1)} %get-tuple-element.21), channel_id=1, source_target_pairs={{0,48},{16,0},{32,16},{48,32},{1,49},{17,1},{33,17},{49,33},{2,50}... | collective-permute-start | bytes 1572872 | tf_op jit(solution)/shard_map/ppermute | solution.py:100
  180.3 33.7 %collective-permute-start.10 = (f32[256,512]{1,0:T(8,128)S(1)}, f32[256,512]{1,0:T(8,128)S(1)}, u32[]{:S(2)}, u32[]{:S(2)}) collective-permute-start(f32[256,512]{1,0:T(8,128)S(1)} %get-tuple-element.34), channel_id=1, source_target_pairs={{0,48},{16,0},{32,16},{48,32},{1,49},{17,1},{33,17},{49,33},{2,50}... | collective-permute-start | bytes 1572872 | tf_op jit(solution)/shard_map/ppermute | solution.py:100
  182.3 31.7 %collective-permute-start.8 = (f32[256,512]{1,0:T(8,128)S(1)}, f32[256,512]{1,0:T(8,128)S(1)}, u32[]{:S(2)}, u32[]{:S(2)}) collective-permute-start(f32[256,512]{1,0:T(8,128)S(1)} %get-tuple-element.33), channel_id=1, source_target_pairs={{0,16},{16,32},{32,48},{48,0},{1,17},{17,33},{33,49},{49,1},{2,18}... | collective-permute-start | bytes 1572872 | tf_op jit(solution)/shard_map/ppermute | solution.py:100
  191.6 31.4 %collective-permute-start.9 = (f32[256,512]{1,0:T(8,128)S(1)}, f32[256,512]{1,0:T(8,128)S(1)}, u32[]{:S(2)}, u32[]{:S(2)}) collective-permute-start(f32[256,512]{1,0:T(8,128)S(1)} %get-tuple-element.35), channel_id=1, source_target_pairs={{0,32},{16,48},{32,0},{48,16},{1,33},{17,49},{33,1},{49,17},{2,34}... | collective-permute-start | bytes 1572872 | tf_op jit(solution)/shard_map/ppermute | solution.py:100
  203.2 20.1 %collective-permute-start.30 = (bf16[2,2,512]{2,0,1:T(2,128)(2,1)S(1)}, bf16[2,2,512]{2,0,1:T(2,128)(2,1)S(1)}, u32[]{:S(2)}, u32[]{:S(2)}) collective-permute-start(bf16[2,2,512]{2,0,1:T(2,128)(2,1)S(1)} %pad_maximum_fusion.1), channel_id=1, source_target_pairs={{0,16},{16,32},{32,48},{48,64},{64,80},{80,96},{96,112},{112,128},... | collective-permute-start | bytes 12296 | tf_op jit(solution)/shard_map/ppermute | solution.py:16
  (26 other events, 278.8 us)
Sparse Core Ops, SparseCore 0:
  26.0 28.8 all-gather.6
  56.7 28.2 all-gather.4

commit v3 on v0

--- a/solution.py
+++ b/solution.py
@@ -85,7 +85,7 @@
                 partial = partial + contribution(jnp.where(use_low, low, high), weight)
         partial = partial.reshape(across, tok_rows, width_local)
         total = lax.dynamic_index_in_dim(partial, me_x, axis=0, keepdims=False)
-        for k in range(1, across):
+        for k in sorted(range(1, across), key=lambda k: -min(k, across - k)):
             route = [(i, (i + k) % across) for i in range(across)]
             piece = lax.dynamic_index_in_dim(partial, (me_x + k) % across, axis=0, keepdims=False)
             total = total + lax.ppermute(piece, "x", route)
@@ -131,10 +131,8 @@
         tok_rows, width_local, mode_count
     )
     shrink = jnp.exp(-decay_rate[None, :, :] * position[:, None, None])
-    weighted = residue[None] * shrink
-    inside = jnp.sum(weighted * running_sum, axis=2)
     entering = (incoming * jnp.exp(-decay_rate))[None]
-    convolved = inside + jnp.sum(weighted * entering, axis=2)
+    convolved = jnp.sum(residue[None] * shrink * (running_sum + entering), axis=2)
     long_mix = convolved + skip_gain[None, :] * gated_wide
     query_gate = short_conv(order[-1:])[:, 0]
     return (query_gate * long_mix).astype(jnp.bfloat16)

time: 248 us -> 245 us (0.988)
  waiting for transfers between devices: 111 us -> 108 us
  starting transfers between devices: 84.8 us -> 87.7 us
    ppermute x6, starting transfers between devices: 4.94 us -> 10.6 us  [ring_sends(): received.append(lax.ppermute(pieces(k, position), axis, route))]
    ppermute x2, waiting for transfers between devices: 5.6 us -> 0.01 us  [from_behind(): return lax.ppermute(block, axis, route)]
    ppermute x6, waiting for transfers between devices: 3.01 us -> 6.8 us  [ring_sends(): received.append(lax.ppermute(pieces(k, position), axis, route))]
  transfers between devices with their start and end apart: 38 -> 38, of which waited for: 19 -> 19; matrix products, arithmetic and copies ran while one was open for 12% -> 8% of each run, Pallas kernels for 0% -> 0%
where the time goes in v3:
time: 245 us; the launch traced here: 244 us
  waiting for transfers between devices  108 us (44%)
  starting transfers between devices  87.7 us (36%)
  matrix products  25.9 us (11%)
  between operations  14.1 us (6%)
  other arithmetic  6.39 us (3%)
  local copies, waits for them, and re-layouts  2.65 us (1%)
    ppermute x9, waiting for transfers between devices, block(): total = total + lax.ppermute(piece, 'x', route)  38.3 us
    ppermute x6, waiting for transfers between devices, line_gather(): lax.ppermute(near_a, axis, [(i + 1, i) for i in range(0, size - d)])  32.8 us
    all_gather x1, waiting for transfers between devices, block(): gathered = lax.all_gather(both, ('y', 'c'), axis=0, tiled=False)  21.1 us
    dot_general x15, matrix products, contribution(): jnp.einsum('chru,uk->hcrk', taken, weight, preferred_element_type=jnp.flo...  15.8 us
    ppermute x3, starting transfers between devices, line_gather(): near_b = lax.ppermute(piece, axis, [(i, i + 1) for i in range(size - 1)])  14.6 us
    ppermute x9, starting transfers between devices, block(): total = total + lax.ppermute(piece, 'x', route)  13.8 us
    ppermute x6, starting transfers between devices, line_gather(): lax.ppermute(near_a, axis, [(i + 1, i) for i in range(0, size - d)])  12.9 us
    ppermute x6, starting transfers between devices, line_gather(): lax.ppermute(near_b, axis, [(i, i + 1) for i in range(d - 1, size - 1)])  12.9 us
  transfers between devices with their start and end apart: 38, of which 19 were waited for; matrix products, arithmetic and copies ran while one was open for 8% of the time, Pallas kernels for 0%

profile of v3, /device:TPU:32, one launch (start us, length us, event | category | flops | bytes accessed | tf_op | source)
XLA Modules:
  0.0 244.5 jit_solution(3125924444767831173)
XLA Ops:
  8.3 8.8 %collective-permute-start.1 = (bf16[256,512]{1,0:T(8,128)(2,1)}, bf16[256,512]{1,0:T(8,128)(2,1)S(1)}, u32[]{:S(2)}, u32[]{:S(2)}) collective-permute-start(bf16[256,512]{1,0:T(8,128)(2,1)} %param.6), channel_id=1, source_target_pairs={{0,2},{1,18},{2,34},{3,50},{16,3},{17,19},{18,35},{19,51},{32,0},{... | collective-permute-start | bytes 786440 | tf_op jit(solution)/shard_map/ppermute | solution.py:64
  17.0 7.3 %collective-permute-done.1 = bf16[256,512]{1,0:T(8,128)(2,1)S(1)} collective-permute-done((bf16[256,512]{1,0:T(8,128)(2,1)}, bf16[256,512]{1,0:T(8,128)(2,1)S(1)}, u32[]{:S(2)}, u32[]{:S(2)}) %collective-permute-start.1) | collective-permute-done | bytes 262176 | tf_op jit(solution)/shard_map/ppermute | solution.py:64
  26.6 6.8 %collective-permute-start.12 = (bf16[512,512]{1,0:T(8,128)(2,1)}, bf16[512,512]{1,0:T(8,128)(2,1)}, u32[]{:S(2)}, u32[]{:S(2)}) collective-permute-start(bf16[512,512]{1,0:T(8,128)(2,1)} %get-tuple-element.16), channel_id=1, source_target_pairs={{0,64},{64,128},{128,192},{1,65},{65,129},{129,193},{2,66},{66,130... | collective-permute-start | bytes 1572872 | tf_op jit(solution)/shard_map/ppermute | solution.py:30
  35.3 3.9 %collective-permute-start.21 = (bf16[512,512]{1,0:T(8,128)(2,1)}, bf16[512,512]{1,0:T(8,128)(2,1)S(1)}, u32[]{:S(2)}, u32[]{:S(2)}) collective-permute-start(bf16[512,512]{1,0:T(8,128)(2,1)} %get-tuple-element.18), channel_id=1, source_target_pairs={{0,64},{64,128},{128,192},{1,65},{65,129},{129,193},{2,66},{66,130... | collective-permute-start | bytes 1572872 | tf_op jit(solution)/shard_map/ppermute | solution.py:30
  41.2 3.9 %collective-permute-start.2 = (bf16[512,512]{1,0:T(8,128)(2,1)}, bf16[512,512]{1,0:T(8,128)(2,1)S(1)}, u32[]{:S(2)}, u32[]{:S(2)}) collective-permute-start(bf16[512,512]{1,0:T(8,128)(2,1)} %get-tuple-element.17), channel_id=1, source_target_pairs={{0,64},{64,128},{128,192},{1,65},{65,129},{129,193},{2,66},{66,130... | collective-permute-start | bytes 1572872 | tf_op jit(solution)/shard_map/ppermute | solution.py:30
  45.3 21.1 %all-gather.3.cloned.1.call-done = bf16[16,256,512]{2,1,0:T(8,128)(2,1)} async-done(((bf16[2,256,512]{2,1,0:T(8,128)(2,1)}), bf16[16,256,512]{2,1,0:T(8,128)(2,1)}) %all-gather.3.cloned.1.call-update) | async-done | bytes 4194320 | tf_op jit(solution)/shard_map/all_gather | solution.py:66
  72.9 3.5 %collective-permute-start.14 = (bf16[512,512]{1,0:T(8,128)(2,1)}, bf16[512,512]{1,0:T(8,128)(2,1)S(1)}, u32[]{:S(2)}, u32[]{:S(2)}) collective-permute-start(bf16[512,512]{1,0:T(8,128)(2,1)} %collective-permute-done.12), channel_id=1, source_target_pairs={{64,128},{128,192},{65,129},{129,193},{66,130},{130,194},{67,131},... | collective-permute-start | bytes 1572872 | tf_op jit(solution)/shard_map/ppermute | solution.py:35
  78.3 4.0 %collective-permute-start.23 = (bf16[512,512]{1,0:T(8,128)(2,1)S(1)}, bf16[512,512]{1,0:T(8,128)(2,1)S(1)}, u32[]{:S(2)}, u32[]{:S(2)}) collective-permute-start(bf16[512,512]{1,0:T(8,128)(2,1)S(1)} %collective-permute-done.21), channel_id=1, source_target_pairs={{64,128},{128,192},{65,129},{129,193},{66,130},{130,194},{67,131},... | collective-permute-start | bytes 1572872 | tf_op jit(solution)/shard_map/ppermute | solution.py:35
  87.4 3.3 %collective-permute-start.4 = (bf16[512,512]{1,0:T(8,128)(2,1)S(1)}, bf16[512,512]{1,0:T(8,128)(2,1)S(1)}, u32[]{:S(2)}, u32[]{:S(2)}) collective-permute-start(bf16[512,512]{1,0:T(8,128)(2,1)S(1)} %collective-permute-done.2), channel_id=1, source_target_pairs={{64,128},{128,192},{65,129},{129,193},{66,130},{130,194},{67,131},... | collective-permute-start | bytes 1572872 | tf_op jit(solution)/shard_map/ppermute | solution.py:35
  92.7 6.0 %collective-permute-done.15 = bf16[512,512]{1,0:T(8,128)(2,1)S(1)} collective-permute-done((bf16[512,512]{1,0:T(8,128)(2,1)}, bf16[512,512]{1,0:T(8,128)(2,1)S(1)}, u32[]{:S(2)}, u32[]{:S(2)}) %collective-permute-start.15) | collective-permute-done | bytes 524320 | tf_op jit(solution)/shard_map/ppermute | solution.py:36
  104.2 5.6 %collective-permute-done.24 = bf16[512,512]{1,0:T(8,128)(2,1)S(1)} collective-permute-done((bf16[512,512]{1,0:T(8,128)(2,1)S(1)}, bf16[512,512]{1,0:T(8,128)(2,1)S(1)}, u32[]{:S(2)}, u32[]{:S(2)}) %collective-permute-start.24) | collective-permute-done | bytes 524320 | tf_op jit(solution)/shard_map/ppermute | solution.py:36
  113.0 7.4 %collective-permute-done.5 = bf16[512,512]{1,0:T(8,128)(2,1)S(1)} collective-permute-done((bf16[512,512]{1,0:T(8,128)(2,1)S(1)}, bf16[512,512]{1,0:T(8,128)(2,1)S(1)}, u32[]{:S(2)}, u32[]{:S(2)}) %collective-permute-start.5) | collective-permute-done | bytes 524320 | tf_op jit(solution)/shard_map/ppermute | solution.py:36
  121.0 3.1 %collective-permute-start.7 = (bf16[512,512]{1,0:T(8,128)(2,1)S(1)}, bf16[512,512]{1,0:T(8,128)(2,1)S(1)}, u32[]{:S(2)}, u32[]{:S(2)}) collective-permute-start(bf16[512,512]{1,0:T(8,128)(2,1)S(1)} %collective-permute-done.5), channel_id=1, source_target_pairs={{64,0},{65,1},{66,2},{67,3},{68,4},{69,5},{70,6},{71,7},{72,8},{73... | collective-permute-start | bytes 1572872 | tf_op jit(solution)/shard_map/ppermute | solution.py:36
  124.2 6.1 %collective-permute-done.17 = bf16[512,512]{1,0:T(8,128)(2,1)S(1)} collective-permute-done((bf16[512,512]{1,0:T(8,128)(2,1)S(1)}, bf16[512,512]{1,0:T(8,128)(2,1)S(1)}, u32[]{:S(2)}, u32[]{:S(2)}) %collective-permute-start.17) | collective-permute-done | bytes 524320 | tf_op jit(solution)/shard_map/ppermute | solution.py:36
  131.5 3.1 %collective-permute-start.18 = (f32[256,512]{1,0:T(8,128)S(1)}, f32[256,512]{1,0:T(8,128)S(1)}, u32[]{:S(2)}, u32[]{:S(2)}) collective-permute-start(f32[256,512]{1,0:T(8,128)S(1)} %get-tuple-element.7), channel_id=1, source_target_pairs={{0,32},{16,48},{32,0},{48,16},{1,33},{17,49},{33,1},{49,17},{2,34}... | collective-permute-start | bytes 1572872 | tf_op jit(solution)/shard_map/ppermute | solution.py:91
  138.1 3.5 %collective-permute-done.26 = bf16[512,512]{1,0:T(8,128)(2,1)S(1)} collective-permute-done((bf16[512,512]{1,0:T(8,128)(2,1)S(1)}, bf16[512,512]{1,0:T(8,128)(2,1)S(1)}, u32[]{:S(2)}, u32[]{:S(2)}) %collective-permute-start.26) | collective-permute-done | bytes 524320 | tf_op jit(solution)/shard_map/ppermute | solution.py:36
  147.8 4.2 %collective-permute-done.7 = bf16[512,512]{1,0:T(8,128)(2,1)S(1)} collective-permute-done((bf16[512,512]{1,0:T(8,128)(2,1)S(1)}, bf16[512,512]{1,0:T(8,128)(2,1)S(1)}, u32[]{:S(2)}, u32[]{:S(2)}) %collective-permute-start.7) | collective-permute-done | bytes 524320 | tf_op jit(solution)/shard_map/ppermute | solution.py:36
  159.7 7.5 %collective-permute-done.20 = f32[256,512]{1,0:T(8,128)S(1)} collective-permute-done((f32[256,512]{1,0:T(8,128)S(1)}, f32[256,512]{1,0:T(8,128)S(1)}, u32[]{:S(2)}, u32[]{:S(2)}) %collective-permute-start.20) | collective-permute-done | bytes 524320 | tf_op jit(solution)/shard_map/ppermute | solution.py:91
  172.5 9.2 %collective-permute-done.28 = f32[256,512]{1,0:T(8,128)S(1)} collective-permute-done((f32[256,512]{1,0:T(8,128)S(1)}, f32[256,512]{1,0:T(8,128)S(1)}, u32[]{:S(2)}, u32[]{:S(2)}) %collective-permute-start.28) | collective-permute-done | bytes 524320 | tf_op jit(solution)/shard_map/ppermute | solution.py:91
  181.9 3.4 %collective-permute-start.30 = (bf16[2,2,512]{2,0,1:T(2,128)(2,1)S(1)}, bf16[2,2,512]{2,0,1:T(2,128)(2,1)S(1)}, u32[]{:S(2)}, u32[]{:S(2)}) collective-permute-start(bf16[2,2,512]{2,0,1:T(2,128)(2,1)S(1)} %pad_maximum_fusion.2), channel_id=1, source_target_pairs={{0,16},{16,32},{32,48},{48,64},{64,80},{80,96},{96,112},{112,128},... | collective-permute-start | bytes 12296 | tf_op jit(solution)/shard_map/ppermute | solution.py:16
  185.3 15.8 %collective-permute-done.10 = f32[256,512]{1,0:T(8,128)S(1)} collective-permute-done((f32[256,512]{1,0:T(8,128)S(1)}, f32[256,512]{1,0:T(8,128)S(1)}, u32[]{:S(2)}, u32[]{:S(2)}) %collective-permute-start.10) | collective-permute-done | bytes 524320 | tf_op jit(solution)/shard_map/ppermute | solution.py:91
  205.8 2.9 %collective-permute-start.32 = (f32[512,16]{0,1:T(8,128)S(1)}, f32[512,16]{0,1:T(8,128)S(1)}, u32[]{:S(2)}, u32[]{:S(2)}) collective-permute-start(f32[512,16]{0,1:T(8,128)S(1)} %multiply_reduce_fusion), channel_id=1, source_target_pairs={{0,32},{16,48},{32,0},{48,16},{1,33},{17,49},{33,1},{49,17},{2,34}... | collective-permute-start | bytes 98312 | tf_op jit(solution)/shard_map/ppermute | solution.py:24
  212.8 4.8 %collective-permute-start.35 = (f32[4,512,16]{1,2,0:T(8,128)S(1)}, f32[4,512,16]{1,2,0:T(8,128)S(1)}, u32[]{:S(2)}, u32[]{:S(2)}) collective-permute-start(f32[4,512,16]{1,2,0:T(8,128)S(1)} %get-tuple-element.22), channel_id=1, source_target_pairs={{0,128},{64,192},{128,0},{192,64},{1,129},{65,193},{129,1},{193,65... | collective-permute-start | bytes 393224 | tf_op jit(solution)/shard_map/ppermute | solution.py:24
  226.6 10.1 %multiply_reduce_fusion.1 = f32[256,512]{1,0:T(8,128)S(1)} fusion(f32[512,16]{0,1:T(8,128)S(1)} %exponential_multiply_fusion, f32[512,16]{0,1:T(8,128)S(1)} %neg.8, f32[512,16]{0,1:T(8,128)S(1)} %copy-done.5, f32[512,16,256]{2,1,0:T(8,128)S(1)} %bitcast.266), kind=kOutput, calls=%fused_computation.4 | convolution fusion | flops 6452871168 | bytes 9011200 | tf_op jit(solution)/shard_map/dot_general | solution.py:130
  (117 shorter events, 75.1 us)
Async XLA Ops:
  6.5 59.9 %all-gather.3.cloned.1.call-start = ((), (), s32[]{:S(2)}) async-start(), calls=%async_computation | async-start | bytes 4718592 | tf_op jit(solution)/shard_map/all_gather | solution.py:66
  26.6 43.9 %collective-permute-start.12 = (bf16[512,512]{1,0:T(8,128)(2,1)}, bf16[512,512]{1,0:T(8,128)(2,1)}, u32[]{:S(2)}, u32[]{:S(2)}) collective-permute-start(bf16[512,512]{1,0:T(8,128)(2,1)} %get-tuple-element.16), channel_id=1, source_target_pairs={{0,64},{64,128},{128,192},{1,65},{65,129},{129,193},{2,66},{66,130... | collective-permute-start | bytes 1572872 | tf_op jit(solution)/shard_map/ppermute | solution.py:30
  33.4 39.5 %collective-permute-start.13 = (bf16[512,512]{1,0:T(8,128)(2,1)}, bf16[512,512]{1,0:T(8,128)(2,1)}, u32[]{:S(2)}, u32[]{:S(2)}) collective-permute-start(bf16[512,512]{1,0:T(8,128)(2,1)} %get-tuple-element.16), channel_id=1, source_target_pairs={{64,0},{128,64},{192,128},{65,1},{129,65},{193,129},{66,2},{130,66... | collective-permute-start | bytes 1572872 | tf_op jit(solution)/shard_map/ppermute | solution.py:31
  35.3 41.1 %collective-permute-start.21 = (bf16[512,512]{1,0:T(8,128)(2,1)}, bf16[512,512]{1,0:T(8,128)(2,1)S(1)}, u32[]{:S(2)}, u32[]{:S(2)}) collective-permute-start(bf16[512,512]{1,0:T(8,128)(2,1)} %get-tuple-element.18), channel_id=1, source_target_pairs={{0,64},{64,128},{128,192},{1,65},{65,129},{129,193},{2,66},{66,130... | collective-permute-start | bytes 1572872 | tf_op jit(solution)/shard_map/ppermute | solution.py:30
  39.2 39.1 %collective-permute-start.22 = (bf16[512,512]{1,0:T(8,128)(2,1)}, bf16[512,512]{1,0:T(8,128)(2,1)S(1)}, u32[]{:S(2)}, u32[]{:S(2)}) collective-permute-start(bf16[512,512]{1,0:T(8,128)(2,1)} %get-tuple-element.18), channel_id=1, source_target_pairs={{64,0},{128,64},{192,128},{65,1},{129,65},{193,129},{66,2},{130,66... | collective-permute-start | bytes 1572872 | tf_op jit(solution)/shard_map/ppermute | solution.py:31
  41.2 43.6 %collective-permute-start.2 = (bf16[512,512]{1,0:T(8,128)(2,1)}, bf16[512,512]{1,0:T(8,128)(2,1)S(1)}, u32[]{:S(2)}, u32[]{:S(2)}) collective-permute-start(bf16[512,512]{1,0:T(8,128)(2,1)} %get-tuple-element.17), channel_id=1, source_target_pairs={{0,64},{64,128},{128,192},{1,65},{65,129},{129,193},{2,66},{66,130... | collective-permute-start | bytes 1572872 | tf_op jit(solution)/shard_map/ppermute | solution.py:30
  76.4 22.2 %collective-permute-start.15 = (bf16[512,512]{1,0:T(8,128)(2,1)}, bf16[512,512]{1,0:T(8,128)(2,1)S(1)}, u32[]{:S(2)}, u32[]{:S(2)}) collective-permute-start(bf16[512,512]{1,0:T(8,128)(2,1)} %collective-permute-done.13), channel_id=1, source_target_pairs={{64,0},{128,64},{65,1},{129,65},{66,2},{130,66},{67,3},{131,67},{6... | collective-permute-start | bytes 1572872 | tf_op jit(solution)/shard_map/ppermute | solution.py:36
  84.8 25.1 %collective-permute-start.24 = (bf16[512,512]{1,0:T(8,128)(2,1)S(1)}, bf16[512,512]{1,0:T(8,128)(2,1)S(1)}, u32[]{:S(2)}, u32[]{:S(2)}) collective-permute-start(bf16[512,512]{1,0:T(8,128)(2,1)S(1)} %collective-permute-done.22), channel_id=1, source_target_pairs={{64,0},{128,64},{65,1},{129,65},{66,2},{130,66},{67,3},{131,67},{6... | collective-permute-start | bytes 1572872 | tf_op jit(solution)/shard_map/ppermute | solution.py:36
  87.4 23.2 %collective-permute-start.4 = (bf16[512,512]{1,0:T(8,128)(2,1)S(1)}, bf16[512,512]{1,0:T(8,128)(2,1)S(1)}, u32[]{:S(2)}, u32[]{:S(2)}) collective-permute-start(bf16[512,512]{1,0:T(8,128)(2,1)S(1)} %collective-permute-done.2), channel_id=1, source_target_pairs={{64,128},{128,192},{65,129},{129,193},{66,130},{130,194},{67,131},... | collective-permute-start | bytes 1572872 | tf_op jit(solution)/shard_map/ppermute | solution.py:35
  90.7 29.6 %collective-permute-start.5 = (bf16[512,512]{1,0:T(8,128)(2,1)S(1)}, bf16[512,512]{1,0:T(8,128)(2,1)S(1)}, u32[]{:S(2)}, u32[]{:S(2)}) collective-permute-start(bf16[512,512]{1,0:T(8,128)(2,1)S(1)} %collective-permute-done.3), channel_id=1, source_target_pairs={{64,0},{128,64},{65,1},{129,65},{66,2},{130,66},{67,3},{131,67},{6... | collective-permute-start | bytes 1572872 | tf_op jit(solution)/shard_map/ppermute | solution.py:36
  98.6 22.4 %collective-permute-start.16 = (bf16[512,512]{1,0:T(8,128)(2,1)S(1)}, bf16[512,512]{1,0:T(8,128)(2,1)S(1)}, u32[]{:S(2)}, u32[]{:S(2)}) collective-permute-start(bf16[512,512]{1,0:T(8,128)(2,1)S(1)} %collective-permute-done.14), channel_id=1, source_target_pairs={{128,192},{129,193},{130,194},{131,195},{132,196},{133,197},{134,1... | collective-permute-start | bytes 1572872 | tf_op jit(solution)/shard_map/ppermute | solution.py:35
  100.1 30.2 %collective-permute-start.17 = (bf16[512,512]{1,0:T(8,128)(2,1)S(1)}, bf16[512,512]{1,0:T(8,128)(2,1)S(1)}, u32[]{:S(2)}, u32[]{:S(2)}) collective-permute-start(bf16[512,512]{1,0:T(8,128)(2,1)S(1)} %collective-permute-done.15), channel_id=1, source_target_pairs={{64,0},{65,1},{66,2},{67,3},{68,4},{69,5},{70,6},{71,7},{72,8},{73... | collective-permute-start | bytes 1572872 | tf_op jit(solution)/shard_map/ppermute | solution.py:36
  109.8 27.6 %collective-permute-start.25 = (bf16[512,512]{1,0:T(8,128)(2,1)S(1)}, bf16[512,512]{1,0:T(8,128)(2,1)S(1)}, u32[]{:S(2)}, u32[]{:S(2)}) collective-permute-start(bf16[512,512]{1,0:T(8,128)(2,1)S(1)} %collective-permute-done.23), channel_id=1, source_target_pairs={{128,192},{129,193},{130,194},{131,195},{132,196},{133,197},{134,1... | collective-permute-start | bytes 1572872 | tf_op jit(solution)/shard_map/ppermute | solution.py:35
  110.5 31.0 %collective-permute-start.26 = (bf16[512,512]{1,0:T(8,128)(2,1)S(1)}, bf16[512,512]{1,0:T(8,128)(2,1)S(1)}, u32[]{:S(2)}, u32[]{:S(2)}) collective-permute-start(bf16[512,512]{1,0:T(8,128)(2,1)S(1)} %collective-permute-done.24), channel_id=1, source_target_pairs={{64,0},{65,1},{66,2},{67,3},{68,4},{69,5},{70,6},{71,7},{72,8},{73... | collective-permute-start | bytes 1572872 | tf_op jit(solution)/shard_map/ppermute | solution.py:36
  120.3 26.5 %collective-permute-start.6 = (bf16[512,512]{1,0:T(8,128)(2,1)S(1)}, bf16[512,512]{1,0:T(8,128)(2,1)S(1)}, u32[]{:S(2)}, u32[]{:S(2)}) collective-permute-start(bf16[512,512]{1,0:T(8,128)(2,1)S(1)} %collective-permute-done.4), channel_id=1, source_target_pairs={{128,192},{129,193},{130,194},{131,195},{132,196},{133,197},{134,1... | collective-permute-start | bytes 1572872 | tf_op jit(solution)/shard_map/ppermute | solution.py:35
  121.0 31.0 %collective-permute-start.7 = (bf16[512,512]{1,0:T(8,128)(2,1)S(1)}, bf16[512,512]{1,0:T(8,128)(2,1)S(1)}, u32[]{:S(2)}, u32[]{:S(2)}) collective-permute-start(bf16[512,512]{1,0:T(8,128)(2,1)S(1)} %collective-permute-done.5), channel_id=1, source_target_pairs={{64,0},{65,1},{66,2},{67,3},{68,4},{69,5},{70,6},{71,7},{72,8},{73... | collective-permute-start | bytes 1572872 | tf_op jit(solution)/shard_map/ppermute | solution.py:36
  131.5 22.0 %collective-permute-start.18 = (f32[256,512]{1,0:T(8,128)S(1)}, f32[256,512]{1,0:T(8,128)S(1)}, u32[]{:S(2)}, u32[]{:S(2)}) collective-permute-start(f32[256,512]{1,0:T(8,128)S(1)} %get-tuple-element.7), channel_id=1, source_target_pairs={{0,32},{16,48},{32,0},{48,16},{1,33},{17,49},{33,1},{49,17},{2,34}... | collective-permute-start | bytes 1572872 | tf_op jit(solution)/shard_map/ppermute | solution.py:91
  141.5 25.7 %collective-permute-start.20 = (f32[256,512]{1,0:T(8,128)S(1)}, f32[256,512]{1,0:T(8,128)S(1)}, u32[]{:S(2)}, u32[]{:S(2)}) collective-permute-start(f32[256,512]{1,0:T(8,128)S(1)} %get-tuple-element.8), channel_id=1, source_target_pairs={{0,48},{16,0},{32,16},{48,32},{1,49},{17,1},{33,17},{49,33},{2,50}... | collective-permute-start | bytes 1572872 | tf_op jit(solution)/shard_map/ppermute | solution.py:91
  146.9 23.6 %collective-permute-start.27 = (f32[256,512]{1,0:T(8,128)S(1)}, f32[256,512]{1,0:T(8,128)S(1)}, u32[]{:S(2)}, u32[]{:S(2)}) collective-permute-start(f32[256,512]{1,0:T(8,128)S(1)} %get-tuple-element.10), channel_id=1, source_target_pairs={{0,32},{16,48},{32,0},{48,16},{1,33},{17,49},{33,1},{49,17},{2,34}... | collective-permute-start | bytes 1572872 | tf_op jit(solution)/shard_map/ppermute | solution.py:91
  152.0 29.6 %collective-permute-start.28 = (f32[256,512]{1,0:T(8,128)S(1)}, f32[256,512]{1,0:T(8,128)S(1)}, u32[]{:S(2)}, u32[]{:S(2)}) collective-permute-start(f32[256,512]{1,0:T(8,128)S(1)} %get-tuple-element.12), channel_id=1, source_target_pairs={{0,16},{16,32},{32,48},{48,0},{1,17},{17,33},{33,49},{49,1},{2,18}... | collective-permute-start | bytes 1572872 | tf_op jit(solution)/shard_map/ppermute | solution.py:91
  153.5 28.2 %collective-permute-start.29 = (f32[256,512]{1,0:T(8,128)S(1)}, f32[256,512]{1,0:T(8,128)S(1)}, u32[]{:S(2)}, u32[]{:S(2)}) collective-permute-start(f32[256,512]{1,0:T(8,128)S(1)} %get-tuple-element.11), channel_id=1, source_target_pairs={{0,48},{16,0},{32,16},{48,32},{1,49},{17,1},{33,17},{49,33},{2,50}... | collective-permute-start | bytes 1572872 | tf_op jit(solution)/shard_map/ppermute | solution.py:91
  159.2 41.9 %collective-permute-start.10 = (f32[256,512]{1,0:T(8,128)S(1)}, f32[256,512]{1,0:T(8,128)S(1)}, u32[]{:S(2)}, u32[]{:S(2)}) collective-permute-start(f32[256,512]{1,0:T(8,128)S(1)} %get-tuple-element.14), channel_id=1, source_target_pairs={{0,48},{16,0},{32,16},{48,32},{1,49},{17,1},{33,17},{49,33},{2,50}... | collective-permute-start | bytes 1572872 | tf_op jit(solution)/shard_map/ppermute | solution.py:91
  167.2 33.9 %collective-permute-start.8 = (f32[256,512]{1,0:T(8,128)S(1)}, f32[256,512]{1,0:T(8,128)S(1)}, u32[]{:S(2)}, u32[]{:S(2)}) collective-permute-start(f32[256,512]{1,0:T(8,128)S(1)} %get-tuple-element.13), channel_id=1, source_target_pairs={{0,32},{16,48},{32,0},{48,16},{1,33},{17,49},{33,1},{49,17},{2,34}... | collective-permute-start | bytes 1572872 | tf_op jit(solution)/shard_map/ppermute | solution.py:91
  170.4 31.4 %collective-permute-start.9 = (f32[256,512]{1,0:T(8,128)S(1)}, f32[256,512]{1,0:T(8,128)S(1)}, u32[]{:S(2)}, u32[]{:S(2)}) collective-permute-start(f32[256,512]{1,0:T(8,128)S(1)} %get-tuple-element.15), channel_id=1, source_target_pairs={{0,16},{16,32},{32,48},{48,0},{1,17},{17,33},{33,49},{49,1},{2,18}... | collective-permute-start | bytes 1572872 | tf_op jit(solution)/shard_map/ppermute | solution.py:91
  (20 other events, 273.8 us)
Sparse Core Ops, SparseCore 0:
  25.5 40.9 all-gather.2
